TPU v7x, 256 devices: a whole 4x4x8 slice. The times are simulated.
256 devices in a mesh: tok: 32 (over z, x), tp: 8 (over y, core).
Axes of the slice: x: 4, y: 4, z: 8, core: 2. Of those that a mesh axis runs over, the one named last changes fastest.
Arguments:
- tokens: bfloat16 [16384, 8192], P('tok', 'tp'), may hold values from -6 to 6
- frozen_weight: bfloat16 [8192, 2048], P('tp'), may hold values from -0.0625 to 0.0625
- adapter_down_matrices: bfloat16 [256, 8192, 64], P('tok', 'tp'), may hold values from -0.0625 to 0.0625
- adapter_up_matrices: bfloat16 [256, 64, 2048], P('tok', None, 'tp'), may hold values from -0.75 to 0.75
- adapter_per_block: int32 [1024], P('tok'), may hold values from 0 to 255, as said below
- slot_per_adapter: int32 [256], replicated, may hold values from 0 to 255, as said below
- rank_per_adapter: int32 [256], replicated, may hold values from 16 to 64
- output_gradient: bfloat16 [16384, 2048], P('tok', 'tp'), may hold values from -6 to 6
Outputs:
- projected: bfloat16 [16384, 2048], P('tok', 'tp')
- token_gradient: bfloat16 [16384, 8192], P('tok', 'tp')
- grad_down: float32 [256, 8192, 64], P('tok', 'tp')
- grad_up: float32 [256, 64, 2048], P('tok', None, 'tp')
Inputs may be any that keep to these rules, and one draw needn't show every extreme that they name: `adapter_per_block`: block b covers tokens b * 16 to (b + 1) * 16 - 1. Among the blocks of one index of tok, at most 2 have adapters stored on any one index of tok (slots k with k // 8 equal), and one index of tok receives exactly 2 such blocks from every index. A permutation: adapter a is stored in slot slot_per_adapter[a] of adapter_down_matrices and adapter_up_matrices.
All inputs are finite; a program needn't handle non-finite values.
Results may differ from a plain program's by a relative error of at most 0.0033.
Values may be sent and summed in bfloat16 or wider, within the bound.
No kernel may reach another device: no remote copies, remote signals or barrier semaphores. Data moves between devices by JAX's collectives and lax.ppermute only.
A program may use at most 128 MiB of HBM per device.

v0:
```python
import jax
import jax.numpy as jnp
from jax import lax
from jax.sharding import PartitionSpec as P

ALPHA = 32
BLOCK_TOKENS = 16


def per_device(
    tokens,
    frozen_weight,
    adapter_down_matrices,
    adapter_up_matrices,
    adapter_per_block,
    slot_per_adapter,
    rank_per_adapter,
    output_gradient,
):
    tok_count = lax.axis_size("tok")
    token_rows = tokens.shape[0]
    width_portion = tokens.shape[1]
    column_portion = output_gradient.shape[1]
    block_count = adapter_per_block.shape[0]
    number_adapters = adapter_down_matrices.shape[0]
    rank_ceiling = adapter_down_matrices.shape[2]
    capacity = max(2, 2 * block_count // tok_count)
    storage_position_count = tok_count * capacity
    adapter_total = slot_per_adapter.shape[0]
    weight_cols = frozen_weight
    base_out = lax.psum_scatter(
        lax.dot_general(
            weight_cols, tokens, (((0,), (1,)), ((), ())), preferred_element_type=jnp.float32
        ),
        "tp",
        scatter_dimension=0,
        tiled=True,
    ).T
    adapter_ids = jnp.arange(adapter_total, dtype=jnp.int32)
    matches = adapter_per_block[:, None] == adapter_ids[None, :]
    block_slot = jnp.sum(jnp.where(matches, slot_per_adapter[None, :], 0), axis=1)
    owner_ids = block_slot // number_adapters
    local_index = block_slot % number_adapters
    block_ids = jnp.arange(block_count, dtype=jnp.int32)
    earlier = (owner_ids[:, None] == owner_ids[None, :]) & (block_ids[None, :] < block_ids[:, None])
    position = jnp.sum(earlier.astype(jnp.int32), axis=1)
    destination = owner_ids * capacity + position
    placement = jnp.arange(storage_position_count, dtype=jnp.int32)[:, None] == destination[None, :]
    place_matrix = placement.astype(jnp.bfloat16)
    send_rows = jnp.dot(
        place_matrix,
        tokens.reshape(block_count, BLOCK_TOKENS * width_portion),
        preferred_element_type=jnp.float32,
    ).astype(jnp.bfloat16)
    send_grads = jnp.dot(
        place_matrix,
        output_gradient.reshape(block_count, BLOCK_TOKENS * column_portion),
        preferred_element_type=jnp.float32,
    ).astype(jnp.bfloat16)
    slot_adapter = jnp.sum(jnp.where(placement, local_index[None, :] + 1, 0), axis=1) - 1
    arrived_rows, arrived_grads, arrived_adapter = (
        lax.all_to_all(
            send_rows.reshape(storage_position_count, BLOCK_TOKENS, width_portion),
            "tok",
            split_axis=0,
            concat_axis=0,
            tiled=True,
        ),
        lax.all_to_all(
            send_grads.reshape(storage_position_count, BLOCK_TOKENS, column_portion),
            "tok",
            split_axis=0,
            concat_axis=0,
            tiled=True,
        ),
        lax.all_to_all(slot_adapter, "tok", split_axis=0, concat_axis=0, tiled=True),
    )
    row_total = storage_position_count * BLOCK_TOKENS
    input_row_block = arrived_rows.reshape(row_total, width_portion)
    gradient_row_block = arrived_grads.reshape(row_total, column_portion)
    chosen = arrived_adapter[:, None] == jnp.arange(number_adapters, dtype=jnp.int32)[None, :]
    chosen_rows = jnp.broadcast_to(
        chosen[:, None, :], (storage_position_count, BLOCK_TOKENS, number_adapters)
    ).reshape(row_total, number_adapters)
    chosen_float = chosen_rows.astype(jnp.float32)
    chosen_half = chosen_rows.astype(jnp.bfloat16)
    stored_ids = lax.axis_index("tok") * number_adapters + jnp.arange(
        number_adapters, dtype=jnp.int32
    )
    stored_match = slot_per_adapter[None, :] == stored_ids[:, None]
    stored_rank = jnp.sum(jnp.where(stored_match, rank_per_adapter[None, :], 0), axis=1)
    stored_scale = jnp.where(
        stored_rank > 0, jnp.float32(ALPHA) / jnp.maximum(stored_rank, 1).astype(jnp.float32), 0.0
    )
    row_rank = jnp.sum(jnp.where(chosen_rows, stored_rank[None, :], 0), axis=1)
    scale_per_row = jnp.sum(chosen_float * stored_scale[None, :], axis=1)
    keep_cols = jnp.arange(rank_ceiling, dtype=jnp.int32)[None, :] < row_rank[:, None]
    reduced_every_row = jnp.einsum(
        "ue,meb->umb", input_row_block, adapter_down_matrices, preferred_element_type=jnp.float32
    )
    low_part = jnp.sum(reduced_every_row * chosen_float[:, :, None], axis=1)
    gathered_every_row = jnp.einsum(
        "hs,gbs->hgb", gradient_row_block, adapter_up_matrices, preferred_element_type=jnp.float32
    )
    pull_part = jnp.sum(gathered_every_row * chosen_float[:, :, None], axis=1)
    low_sum, pull_sum = lax.psum((low_part, pull_part), "tp")
    reduced_rows = jnp.where(keep_cols, low_sum, 0.0).astype(jnp.bfloat16)
    reduced_gradient = (scale_per_row[:, None] * jnp.where(keep_cols, pull_sum, 0.0)).astype(
        jnp.bfloat16
    )
    reduced_picked = chosen_half[:, :, None] * reduced_rows[:, None, :]
    gradient_picked = chosen_half[:, :, None] * reduced_gradient[:, None, :]
    adapter_increment = scale_per_row[:, None] * jnp.einsum(
        "hnq,nqs->hs", reduced_picked, adapter_up_matrices, preferred_element_type=jnp.float32
    )
    grad_down = jnp.einsum(
        "rd,rak->adk", input_row_block, gradient_picked, preferred_element_type=jnp.float32
    )
    grad_up = stored_scale[:, None, None] * jnp.einsum(
        "rak,rc->akc", reduced_picked, gradient_row_block, preferred_element_type=jnp.float32
    )
    adapter_output_rows = jnp.einsum(
        "ymf,mcf->yc", gradient_picked, adapter_down_matrices, preferred_element_type=jnp.float32
    )
    delta_back, row_input_gradient = (
        lax.all_to_all(
            adapter_increment.reshape(storage_position_count, BLOCK_TOKENS, column_portion),
            "tok",
            split_axis=0,
            concat_axis=0,
            tiled=True,
        ),
        lax.all_to_all(
            adapter_output_rows.reshape(storage_position_count, BLOCK_TOKENS, width_portion),
            "tok",
            split_axis=0,
            concat_axis=0,
            tiled=True,
        ),
    )
    adapter_input_gradient = jnp.take(row_input_gradient, destination, axis=0)
    mine_delta = jnp.take(delta_back, destination, axis=0)
    projected = (base_out + mine_delta.reshape(token_rows, column_portion)).astype(jnp.bfloat16)
    weight_cols = frozen_weight
    frozen_input_gradient = lax.dot_general(
        lax.all_gather(output_gradient, "tp", axis=1, tiled=True),
        weight_cols,
        (((1,), (1,)), ((), ())),
        preferred_element_type=jnp.float32,
    )
    token_gradient = (
        frozen_input_gradient + adapter_input_gradient.reshape(token_rows, width_portion)
    ).astype(jnp.bfloat16)
    return (projected, token_gradient, grad_down, grad_up)


def solution(mesh):
    return jax.shard_map(
        per_device,
        mesh=mesh,
        in_specs=(
            P("tok", "tp"),
            P("tp", None),
            P("tok", "tp", None),
            P("tok", None, "tp"),
            P("tok"),
            P(),
            P(),
            P("tok", "tp"),
        ),
        out_specs=(P("tok", "tp"), P("tok", "tp"), P("tok", "tp", None), P("tok", None, "tp")),
        check_vma=False,
    )
```

profile of v0, /device:TPU:27, one launch (start us, length us, event | category | flops | bytes accessed | tf_op | source)
XLA Modules:
  0.0 281.1 jit_solution(14882699248687537473)
XLA Ops:
  7.2 1.0 select_reduce_fusion.2
  9.2 11.1 %all-to-all-start = ((s32[32,2,1]{1,2,0:T(1,128)}), s32[32,2,1]{1,2,0:T(1,128)S(1)}, u32[]{:S(2)}, u32[]{:S(2)}) async-start(s32[32,2,1]{1,2,0:T(1,128)} %bitcast.1), calls=%async_computation.1 | async-start | bytes 32768 | tf_op jit(solution)/shard_map/all_to_all | solution.py:76
  20.3 1.1 reshape.244
  22.7 5.2 %all-to-all-done = s32[32,2,1]{1,2,0:T(1,128)S(1)} async-done(((s32[32,2,1]{1,2,0:T(1,128)}), s32[32,2,1]{1,2,0:T(1,128)S(1)}, u32[]{:S(2)}, u32[]{:S(2)}) %all-to-all-start) | async-done | bytes 288 | tf_op jit(solution)/shard_map/all_to_all | solution.py:76
  27.9 5.4 %all-to-all-start.3 = ((bf16[64,16,256]{2,1,0:T(8,128)(2,1)}), bf16[64,16,256]{2,1,0:T(8,128)(2,1)}, u32[]{:S(2)}, u32[]{:S(2)}) async-start(bf16[64,16,256]{2,1,0:T(8,128)(2,1)} %bitcast.28), calls=%async_computation.4 | async-start | bytes 1048576 | tf_op jit(solution)/shard_map/all_to_all | solution.py:69
  34.6 2.5 copy.26
  37.2 10.8 %all-to-all-done.3 = bf16[64,16,256]{2,1,0:T(8,128)(2,1)} async-done(((bf16[64,16,256]{2,1,0:T(8,128)(2,1)}), bf16[64,16,256]{2,1,0:T(8,128)(2,1)}, u32[]{:S(2)}, u32[]{:S(2)}) %all-to-all-start.3) | async-done | bytes 524320 | tf_op jit(solution)/shard_map/all_to_all | solution.py:69
  48.0 6.5 %all-to-all-start.1 = ((bf16[64,16,1024]{2,1,0:T(8,128)(2,1)}), bf16[64,16,1024]{2,1,0:T(8,128)(2,1)S(1)}, u32[]{:S(2)}, u32[]{:S(2)}) async-start(bf16[64,16,1024]{2,1,0:T(8,128)(2,1)} %bitcast.25), calls=%async_computation.2 | async-start | bytes 4194304 | tf_op jit(solution)/shard_map/all_to_all | solution.py:62
  56.2 2.3 multiply_reduce_fusion
  58.6 6.8 %fusion.34 = f32[2048,512]{1,0:T(8,128)} fusion(bf16[1024,2048]{1,0:T(8,128)(2,1)} %param.9, bf16[512,1024]{1,0:T(8,128)(2,1)} %param.8), kind=kOutput, calls=%fused_computation.69 | convolution fusion | flops 2147483648 | bytes 9437184 | tf_op jit(solution)/shard_map/dot_general | solution.py:32
  67.1 35.0 %all-to-all-done.1 = bf16[64,16,1024]{2,1,0:T(8,128)(2,1)S(1)} async-done(((bf16[64,16,1024]{2,1,0:T(8,128)(2,1)}), bf16[64,16,1024]{2,1,0:T(8,128)(2,1)S(1)}, u32[]{:S(2)}, u32[]{:S(2)}) %all-to-all-start.1) | async-done | bytes 2097184 | tf_op jit(solution)/shard_map/all_to_all | solution.py:62
  102.1 1.3 fusion.35
  103.7 26.9 %all-reduce.4 = bf16[1024,64]{0,1:T(8,128)(2,1)S(1)} all-reduce(f32[1024,64]{0,1:T(8,128)S(1)} %multiply_reduce_fusion.1), channel_id=1, replica_groups=mesh['tok'=32,'tp'=8] {'tp'}, use_global_device_ids=true, to_apply=%region_8.9 | all-reduce | flops 65536 | bytes 393216 | tf_op jit(solution)/shard_map/psum | solution.py:106
  130.6 1.5 fusion.12
  132.1 6.1 %all-to-all-start.2 = ((f32[64,16,256]{2,1,0:T(8,128)}), f32[64,16,256]{2,1,0:T(8,128)S(1)}, u32[]{:S(2)}, u32[]{:S(2)}) async-start(f32[64,16,256]{2,1,0:T(8,128)} %bitcast.7), calls=%async_computation.3 | async-start | bytes 2097152 | tf_op jit(solution)/shard_map/all_to_all | solution.py:126
  139.2 3.3 %fusion.3 = f32[1024,1024,1]{1,0,2:T(8,128)} fusion(bf16[8,1024,64]{1,2,0:T(8,128)(2,1)S(1)} %copy-done, bf16[1024,64]{0,1:T(8,128)(2,1)S(1)} %multiply_convert_fusion, bf16[1024,8]{0,1:T(8,128)(2,1)S(1)} %convert_element_type.58), kind=kOutput, calls=%fused_computation.11 | convolution fusion | flops 1074266112 | bytes 5390336 | tf_op jit(solution)/shard_map/ymf,mcf->yc/dot_general | solution.py:122
  142.5 23.8 %all-to-all-done.2 = f32[64,16,256]{2,1,0:T(8,128)S(1)} async-done(((f32[64,16,256]{2,1,0:T(8,128)}), f32[64,16,256]{2,1,0:T(8,128)S(1)}, u32[]{:S(2)}, u32[]{:S(2)}) %all-to-all-start.2) | async-done | bytes 1048608 | tf_op jit(solution)/shard_map/all_to_all | solution.py:126
  166.3 5.3 %all-to-all-start.4 = ((f32[64,16,1024]{2,1,0:T(8,128)}), f32[64,16,1024]{2,1,0:T(8,128)}, u32[]{:S(2)}, u32[]{:S(2)}) async-start(f32[64,16,1024]{2,1,0:T(8,128)} %bitcast.73), calls=%async_computation.5 | async-start | bytes 8388608 | tf_op jit(solution)/shard_map/all_to_all | solution.py:133
  172.5 2.3 fusion.15
  174.8 4.2 %convolution_bitcast_fusion = f32[8,1024,64]{1,2,0:T(8,128)} fusion(bf16[1024,1024,1]{1,0,2:T(8,128)(2,1)} %bitcast.76, bf16[1024,64]{0,1:T(8,128)(2,1)S(1)} %multiply_convert_fusion, bf16[1024,8]{0,1:T(8,128)(2,1)S(1)} %convert_element_type.58), kind=kOutput, calls=%fused_computation.9 | convolution fusion | flops 1074266112 | bytes 4341760 | tf_op jit(solution)/shard_map/rd,rak->adk/dot_general | solution.py:116
  179.8 1.1 fusion.18
  181.8 83.7 %all-to-all-done.4 = f32[64,16,1024]{2,1,0:T(8,128)} async-done(((f32[64,16,1024]{2,1,0:T(8,128)}), f32[64,16,1024]{2,1,0:T(8,128)}, u32[]{:S(2)}, u32[]{:S(2)}) %all-to-all-start.4) | async-done | bytes 4194336 | tf_op jit(solution)/shard_map/all_to_all | solution.py:133
  265.5 2.9 %gather_fusion.1 = f32[32,16,1024]{2,1,0:T(8,128)S(1)} fusion(f32[64,16,1024]{2,1,0:T(8,128)} %all-to-all-done.4, s32[1024]{0:T(1024)S(1)} %pad_clamp_fusion), kind=kCustom, calls=%fused_computation.1 | custom fusion | bytes 4194432 | tf_op jit(solution)/shard_map/jit(_take)/gather | solution.py:141
  268.5 6.2 %fusion.1 = bf16[512,1024]{1,0:T(8,128)(2,1)} fusion(f32[32,16,1024]{2,1,0:T(8,128)S(1)} %gather_fusion.1, bf16[512,2048]{1,0:T(8,128)(2,1)} %all-gather.2.cloned.1.call-done, bf16[1024,2048]{1,0:T(8,128)(2,1)} %param.9, pred[512]{0:T(512)(128)(4,1)S(1)} %broadcast_in_dim.122), kind=kOutput, calls=%fused_computation.6 | convolution fusion | flops 2149056512 | bytes 9437696 | tf_op jit(solution)/shard_map/dot_general | solution.py:145
  (58 shorter events, 11.0 us)
Async XLA Ops:
  7.2 94.9 %copy-start = (bf16[8,1024,64]{1,2,0:T(8,128)(2,1)S(1)}, bf16[8,1024,64]{1,2,0:T(8,128)(2,1)}, u32[]{:S(2)}) copy-start(bf16[8,1024,64]{1,2,0:T(8,128)(2,1)} %param.10) | copy-start | bytes 3145732
  7.2 26.1 %copy-start.2 = (bf16[512,1024]{1,0:T(8,128)(2,1)S(1)}, bf16[512,1024]{1,0:T(8,128)(2,1)}, u32[]{:S(2)}) copy-start(bf16[512,1024]{1,0:T(8,128)(2,1)} %param.8) | copy-start | bytes 3145732
  9.2 18.7 %all-to-all-start = ((s32[32,2,1]{1,2,0:T(1,128)}), s32[32,2,1]{1,2,0:T(1,128)S(1)}, u32[]{:S(2)}, u32[]{:S(2)}) async-start(s32[32,2,1]{1,2,0:T(1,128)} %bitcast.1), calls=%async_computation.1 | async-start | bytes 32768 | tf_op jit(solution)/shard_map/all_to_all | solution.py:76
  27.9 20.1 %all-to-all-start.3 = ((bf16[64,16,256]{2,1,0:T(8,128)(2,1)}), bf16[64,16,256]{2,1,0:T(8,128)(2,1)}, u32[]{:S(2)}, u32[]{:S(2)}) async-start(bf16[64,16,256]{2,1,0:T(8,128)(2,1)} %bitcast.28), calls=%async_computation.4 | async-start | bytes 1048576 | tf_op jit(solution)/shard_map/all_to_all | solution.py:69
  48.0 54.1 %all-to-all-start.1 = ((bf16[64,16,1024]{2,1,0:T(8,128)(2,1)}), bf16[64,16,1024]{2,1,0:T(8,128)(2,1)S(1)}, u32[]{:S(2)}, u32[]{:S(2)}) async-start(bf16[64,16,1024]{2,1,0:T(8,128)(2,1)} %bitcast.25), calls=%async_computation.2 | async-start | bytes 4194304 | tf_op jit(solution)/shard_map/all_to_all | solution.py:62
  54.6 83.6 %all-reduce.3.cloned.1.call-start = ((), (), s32[]{:S(2)}) async-start(), calls=%async_computation.8 | async-start | bytes 524288 | tf_op jit(solution)/shard_map/psum | solution.py:106
  58.5 121.3 %reduce-scatter.2.cloned.1.call-start = ((), (), s32[]{:S(2)}) async-start(), calls=%async_computation.6 | async-start | bytes 4718592 | tf_op jit(solution)/shard_map/reduce_scatter | solution.py:31
  65.4 0.7 copy-start.3
  65.4 0.7 copy-start.4
  102.1 1.3 copy-start.1
  103.4 27.2 %copy-start.5 = (bf16[8,64,256]{2,1,0:T(8,128)(2,1)S(1)}, bf16[8,64,256]{2,1,0:T(8,128)(2,1)}, u32[]{:S(2)}) copy-start(bf16[8,64,256]{2,1,0:T(8,128)(2,1)} %param.11) | copy-start | bytes 786436
  132.1 34.2 %all-to-all-start.2 = ((f32[64,16,256]{2,1,0:T(8,128)}), f32[64,16,256]{2,1,0:T(8,128)S(1)}, u32[]{:S(2)}, u32[]{:S(2)}) async-start(f32[64,16,256]{2,1,0:T(8,128)} %bitcast.7), calls=%async_computation.3 | async-start | bytes 2097152 | tf_op jit(solution)/shard_map/all_to_all | solution.py:126
  166.3 99.3 %all-to-all-start.4 = ((f32[64,16,1024]{2,1,0:T(8,128)}), f32[64,16,1024]{2,1,0:T(8,128)}, u32[]{:S(2)}, u32[]{:S(2)}) async-start(f32[64,16,1024]{2,1,0:T(8,128)} %bitcast.73), calls=%async_computation.5 | async-start | bytes 8388608 | tf_op jit(solution)/shard_map/all_to_all | solution.py:133
  171.6 96.8 %all-gather.2.cloned.1.call-start = ((), (), s32[]{:S(2)}) async-start(), calls=%async_computation.7 | async-start | bytes 2359296 | tf_op jit(solution)/shard_map/all_gather | solution.py:146
Sparse Core Ops, SparseCore 0:
  58.7 67.4 all-reduce.2
  128.7 39.7 reduce-scatter.1
  174.2 30.7 all-gather.1
where the time goes:
time: 283 us; the launch traced here: 281 us
  waiting for transfers between devices  159 us (56%)
  starting transfers between devices  34.5 us (12%)
  matrix products  29 us (10%)
  blocking collectives  26.9 us (10%)
  between operations  14 us (5%)
  local copies, waits for them, and re-layouts  12.7 us (4%)
  other arithmetic  4.8 us (2%)
    all_to_all x1, waiting for transfers between devices, per_device(): lax.all_to_all(adapter_output_rows.reshape(storage_position_count, BLOCK_...  83.7 us
    all_to_all x1, waiting for transfers between devices, per_device(): lax.all_to_all(send_rows.reshape(storage_position_count, BLOCK_TOKENS, wi...  35 us
    psum x1, blocking collectives, per_device(): low_sum, pull_sum = lax.psum((low_part, pull_part), 'tp')  26.9 us
    all_to_all x1, waiting for transfers between devices, per_device(): lax.all_to_all(adapter_increment.reshape(storage_position_count, BLOCK_TO...  23.8 us
    all_to_all x1, starting transfers between devices, per_device(): lax.all_to_all(slot_adapter, 'tok', split_axis=0, concat_axis=0, tiled=True)  11.1 us
    all_to_all x1, waiting for transfers between devices, per_device(): lax.all_to_all(send_grads.reshape(storage_position_count, BLOCK_TOKENS, c...  10.8 us
    dot_general x1, matrix products, per_device(): lax.dot_general(weight_cols, tokens, (((0,), (1,)), ((), ())), preferred_...  6.81 us
    all_to_all x1, starting transfers between devices, per_device(): lax.all_to_all(send_rows.reshape(storage_position_count, BLOCK_TOKENS, wi...  6.54 us
  transfers between devices with their start and end apart: 8, of which 5 were waited for; matrix products, arithmetic and copies ran while one was open for 13% of the time, Pallas kernels for 0%

commit v1 on v0

v1 whole, which is shorter than its diff:
```python
import jax
import jax.numpy as jnp
from jax import lax
from jax.sharding import PartitionSpec as P

ALPHA = 32
BLOCK_TOKENS = 16


def route(block_slot, number_adapters, capacity):
    owner_ids = block_slot // number_adapters
    block_ids = jnp.arange(block_slot.shape[-1], dtype=jnp.int32)
    earlier = (owner_ids[..., :, None] == owner_ids[..., None, :]) & (
        block_ids[None, :] < block_ids[:, None]
    )
    position = jnp.sum(earlier.astype(jnp.int32), axis=-1)
    return owner_ids * capacity + position


def per_device(
    tokens,
    frozen_weight,
    adapter_down_matrices,
    adapter_up_matrices,
    adapter_per_block,
    slot_per_adapter,
    rank_per_adapter,
    output_gradient,
):
    tok_count = lax.axis_size("tok")
    me = lax.axis_index("tok")
    token_rows, width_portion = tokens.shape
    column_portion = output_gradient.shape[1]
    block_count = adapter_per_block.shape[0]
    number_adapters, _, rank_ceiling = adapter_down_matrices.shape
    capacity = max(2, 2 * block_count // tok_count)
    slots = tok_count * capacity
    row_total = slots * BLOCK_TOKENS
    lane = width_portion + column_portion

    block_slot = jnp.take(slot_per_adapter, adapter_per_block)
    destination = route(block_slot, number_adapters, capacity)
    slot_ids = jnp.arange(slots, dtype=jnp.int32)
    hit = destination[None, :] == slot_ids[:, None]
    filled = jnp.any(hit, axis=1)
    source_block = jnp.sum(jnp.where(hit, jnp.arange(block_count, dtype=jnp.int32)[None, :], 0), axis=1)

    packed = jnp.concatenate(
        [
            tokens.reshape(block_count, BLOCK_TOKENS, width_portion),
            output_gradient.reshape(block_count, BLOCK_TOKENS, column_portion),
        ],
        axis=2,
    )
    send = jnp.where(filled[:, None, None], jnp.take(packed, source_block, axis=0), 0)
    arrived = lax.all_to_all(send, "tok", split_axis=0, concat_axis=0, tiled=True)

    all_blocks = lax.all_gather(adapter_per_block, "tok", axis=0, tiled=False)
    all_slot = jnp.take(slot_per_adapter, all_blocks)
    all_dest = route(all_slot, number_adapters, capacity)
    here = all_dest[:, :, None] == (me * capacity + jnp.arange(capacity, dtype=jnp.int32))[None, None, :]
    slot_local = jnp.where(here, (all_slot % number_adapters)[:, :, None] + 1, 0).sum(axis=1) - 1
    slot_adapter = slot_local.reshape(slots)

    input_rows = arrived[:, :, :width_portion].reshape(row_total, width_portion)
    grad_rows = arrived[:, :, width_portion:].reshape(row_total, column_portion)

    stored_ids = me * number_adapters + jnp.arange(number_adapters, dtype=jnp.int32)
    stored_match = slot_per_adapter[None, :] == stored_ids[:, None]
    stored_rank = jnp.sum(jnp.where(stored_match, rank_per_adapter[None, :], 0), axis=1)
    stored_scale = jnp.where(
        stored_rank > 0, jnp.float32(ALPHA) / jnp.maximum(stored_rank, 1).astype(jnp.float32), 0.0
    )
    chosen = slot_adapter[:, None] == jnp.arange(number_adapters, dtype=jnp.int32)[None, :]
    chosen_rows = jnp.broadcast_to(
        chosen[:, None, :], (slots, BLOCK_TOKENS, number_adapters)
    ).reshape(row_total, number_adapters)
    chosen_float = chosen_rows.astype(jnp.float32)
    row_rank = jnp.sum(jnp.where(chosen_rows, stored_rank[None, :], 0), axis=1)
    scale_per_row = jnp.sum(chosen_float * stored_scale[None, :], axis=1)
    keep_cols = jnp.arange(rank_ceiling, dtype=jnp.int32)[None, :] < row_rank[:, None]

    reduced_every_row = jnp.einsum(
        "ue,meb->umb", input_rows, adapter_down_matrices, preferred_element_type=jnp.float32
    )
    low_part = jnp.sum(reduced_every_row * chosen_float[:, :, None], axis=1)
    gathered_every_row = jnp.einsum(
        "hs,gbs->hgb", grad_rows, adapter_up_matrices, preferred_element_type=jnp.float32
    )
    pull_part = jnp.sum(gathered_every_row * chosen_float[:, :, None], axis=1)
    both = lax.psum(jnp.concatenate([low_part, pull_part], axis=1), "tp")
    low_sum = both[:, :rank_ceiling]
    pull_sum = both[:, rank_ceiling:]
    reduced_rows = jnp.where(keep_cols, low_sum, 0.0).astype(jnp.bfloat16)
    reduced_gradient = (scale_per_row[:, None] * jnp.where(keep_cols, pull_sum, 0.0)).astype(
        jnp.bfloat16
    )
    chosen_half = chosen_rows.astype(jnp.bfloat16)
    reduced_picked = chosen_half[:, :, None] * reduced_rows[:, None, :]
    gradient_picked = chosen_half[:, :, None] * reduced_gradient[:, None, :]
    adapter_increment = scale_per_row[:, None] * jnp.einsum(
        "hnq,nqs->hs", reduced_picked, adapter_up_matrices, preferred_element_type=jnp.float32
    )
    grad_down = jnp.einsum(
        "rd,rak->adk", input_rows, gradient_picked, preferred_element_type=jnp.float32
    )
    grad_up = stored_scale[:, None, None] * jnp.einsum(
        "rak,rc->akc", reduced_picked, grad_rows, preferred_element_type=jnp.float32
    )
    adapter_output_rows = jnp.einsum(
        "ymf,mcf->yc", gradient_picked, adapter_down_matrices, preferred_element_type=jnp.float32
    )
    back = jnp.concatenate(
        [
            adapter_output_rows.reshape(slots, BLOCK_TOKENS, width_portion),
            adapter_increment.reshape(slots, BLOCK_TOKENS, column_portion),
        ],
        axis=2,
    )
    returned = lax.all_to_all(back, "tok", split_axis=0, concat_axis=0, tiled=True)
    mine = jnp.take(returned, destination, axis=0)

    base_out = lax.psum_scatter(
        lax.dot_general(
            frozen_weight, tokens, (((0,), (1,)), ((), ())), preferred_element_type=jnp.float32
        ),
        "tp",
        scatter_dimension=0,
        tiled=True,
    ).T
    frozen_input_gradient = lax.dot_general(
        lax.all_gather(output_gradient, "tp", axis=1, tiled=True),
        frozen_weight,
        (((1,), (1,)), ((), ())),
        preferred_element_type=jnp.float32,
    )
    projected = (
        base_out + mine[:, :, width_portion:].reshape(token_rows, column_portion)
    ).astype(jnp.bfloat16)
    token_gradient = (
        frozen_input_gradient + mine[:, :, :width_portion].reshape(token_rows, width_portion)
    ).astype(jnp.bfloat16)
    return (projected, token_gradient, grad_down, grad_up)


def solution(mesh):
    return jax.shard_map(
        per_device,
        mesh=mesh,
        in_specs=(
            P("tok", "tp"),
            P("tp", None),
            P("tok", "tp", None),
            P("tok", None, "tp"),
            P("tok"),
            P(),
            P(),
            P("tok", "tp"),
        ),
        out_specs=(P("tok", "tp"), P("tok", "tp"), P("tok", "tp", None), P("tok", None, "tp")),
        check_vma=False,
    )
```

time: 283 us -> 339 us (1.20)
  blocking collectives: 26.9 us -> 61.4 us
  waiting for transfers between devices: 159 us -> 175 us
  local copies, waits for them, and re-layouts: 12.7 us -> 26.4 us
  starting transfers between devices: 34.5 us -> 21.2 us
  other arithmetic: 4.8 us -> 16.6 us
  matrix products: 29 us -> 22.5 us
    unnamed x0 -> x1, blocking collectives: none -> 61.4 us
    psum x1, waiting for transfers between devices: 0.02 us -> 57.9 us  [per_device(): both = lax.psum(jnp.concatenate([low_part, pull_part], axis=1), 'tp')]
    all_to_all x5 -> x2, waiting for transfers between devices: 159 us -> 117 us  [the longest x1 117 us: per_device(): lax.all_to_all(back, 'tok', split_axis=0, concat_axis=0, tiled=True)]
    psum x1 -> x0, blocking collectives: 26.9 us -> none  [per_device(): low_sum, pull_sum = lax.psum((low_part, pull_part), 'tp')]
    all_to_all x5 -> x2, starting transfers between devices: 34.4 us -> 20.9 us  [the longest x1 11.2 us: per_device(): lax.all_to_all(send, 'tok', split_axis=0, concat_axis=0, tiled=True)]
    gather x3 -> x5, local copies, waits for them, and re-layouts: 3.65 us -> 15.2 us  [the longest x2 6.9 us: per_device(): all_slot = jnp.take(slot_per_adapter, all_blocks)]
    select_n x1 -> x8, other arithmetic: 0.01 us -> 7.09 us  [the longest x1 3.66 us: per_device(): jnp.where(filled[:, None, None], jnp.take(packed, source_block, axis=0), 0)]
    concatenate x0 -> x3, other arithmetic: none -> 5.11 us  [the longest x1 2.85 us: per_device(): jnp.concatenate([adapter_output_rows.reshape(slots, BLOCK_TOKENS, width_p...]
  transfers between devices with their start and end apart: 8 -> 5, of which waited for: 5 -> 2; matrix products, arithmetic and copies ran while one was open for 13% -> 12% of each run, Pallas kernels for 0% -> 0%
where the time goes in v1:
time: 339 us; the launch traced here: 338 us
  waiting for transfers between devices  175 us (52%)
  blocking collectives  61.4 us (18%)
  local copies, waits for them, and re-layouts  26.4 us (8%)
  matrix products  22.5 us (7%)
  starting transfers between devices  21.2 us (6%)
  other arithmetic  16.6 us (5%)
  between operations  14.7 us (4%)
    all_to_all x1, waiting for transfers between devices, per_device(): lax.all_to_all(back, 'tok', split_axis=0, concat_axis=0, tiled=True)  117 us
    unnamed x1, blocking collectives  61.4 us
    psum x1, waiting for transfers between devices, per_device(): both = lax.psum(jnp.concatenate([low_part, pull_part], axis=1), 'tp')  57.9 us
    all_to_all x1, starting transfers between devices, per_device(): lax.all_to_all(send, 'tok', split_axis=0, concat_axis=0, tiled=True)  11.2 us
    all_to_all x1, starting transfers between devices, per_device(): lax.all_to_all(back, 'tok', split_axis=0, concat_axis=0, tiled=True)  9.63 us
    dot_general x1, matrix products, per_device(): lax.dot_general(frozen_weight, tokens, (((0,), (1,)), ((), ())), preferre...  6.97 us
    gather x2, local copies, waits for them, and re-layouts, per_device(): all_slot = jnp.take(slot_per_adapter, all_blocks)  6.9 us
  transfers between devices with their start and end apart: 5, of which 2 were waited for; matrix products, arithmetic and copies ran while one was open for 12% of the time, Pallas kernels for 0%

profile of v1, /device:TPU:27, one launch (start us, length us, event | category | flops | bytes accessed | tf_op | source)
XLA Modules:
  0.0 338.1 jit_solution(13137650032125103438)
XLA Ops:
  7.9 1.4 gather_fusion
  10.4 1.4 pad_maximum_fusion.1
  11.8 2.2 gather_fusion.2
  14.1 3.7 %select_select_fusion = bf16[64,16,1280]{2,1,0:T(8,128)(2,1)} fusion(bf16[64,16,1280]{2,1,0:T(8,128)(2,1)} %gather_fusion.2, pred[64]{0:T(512)(128)(4,1)S(1)} %compare_and_fusion, pred[64]{0:T(512)(128)(4,1)S(1)} %fusion.30), kind=kLoop, calls=%fused_computation.5 | loop fusion | flops 2621440 | bytes 5243008 | tf_op jit(solution)/shard_map/jit(_where)/select_n | solution.py:55
  17.7 11.2 %all-to-all-start = ((bf16[64,16,1280]{2,1,0:T(8,128)(2,1)}), bf16[64,16,1280]{2,1,0:T(8,128)(2,1)}, u32[]{:S(2)}, u32[]{:S(2)}) async-start(bf16[64,16,1280]{2,1,0:T(8,128)(2,1)} %select_select_fusion), calls=%async_computation.1 | async-start | bytes 5242880 | tf_op jit(solution)/shard_map/all_to_all | solution.py:56
  30.5 61.4 %all-reduce = s32[1024]{0:T(1024)S(1)} all-reduce(s32[1024]{0:T(1024)S(1)} %dynamic-update-slice), channel_id=2, replica_groups=mesh['tok'=32,'tp'=8] {'tok'}, use_global_device_ids=true, to_apply=%add | all-reduce | flops 1024 | bytes 8192
  92.1 6.8 %gather_fusion.1 = s32[1024]{0:T(1024)S(1)} fusion(s32[256]{0:T(256)S(1)} %copy-done.1, s32[1024]{0:T(1024)S(1)} %broadcast_clamp_fusion), kind=kCustom, calls=%fused_computation.1 | custom fusion | bytes 12288 | tf_op jit(solution)/shard_map/jit(_take)/gather | solution.py:59
  100.6 1.8 slice.32
  102.5 1.3 fusion.37
  104.0 1.1 slice.33
  107.3 7.0 %fusion.36 = f32[2048,512]{1,0:T(8,128)} fusion(bf16[1024,2048]{1,0:T(8,128)(2,1)} %param.9, bf16[512,1024]{1,0:T(8,128)(2,1)} %param.8), kind=kOutput, calls=%fused_computation.86 | convolution fusion | flops 2147483648 | bytes 9437184 | tf_op jit(solution)/shard_map/dot_general | solution.py:124
  116.0 57.9 %all-reduce.3.cloned.1.call-done = f32[1024,128]{0,1:T(8,128)} async-done(((f32[1024,128]{0,1:T(8,128)}), f32[1024,128]{0,1:T(8,128)}) %all-reduce.3.cloned.1.call-update) | async-done | bytes 524304 | tf_op jit(solution)/shard_map/psum | solution.py:91
  174.9 1.5 fusion.11
  176.4 1.3 fusion.6
  177.7 2.9 pad_maximum_fusion
  180.6 9.6 %all-to-all-start.1 = ((f32[64,16,1280]{2,1,0:T(8,128)}), f32[64,16,1280]{2,1,0:T(8,128)}, u32[]{:S(2)}, u32[]{:S(2)}) async-start(f32[64,16,1280]{2,1,0:T(8,128)} %pad_maximum_fusion), calls=%async_computation.2 | async-start | bytes 10485760 | tf_op jit(solution)/shard_map/all_to_all | solution.py:120
  191.0 2.3 fusion.14
  193.3 2.6 convolution_bitcast_fusion
  195.9 116.9 %all-to-all-done.1 = f32[64,16,1280]{2,1,0:T(8,128)} async-done(((f32[64,16,1280]{2,1,0:T(8,128)}), f32[64,16,1280]{2,1,0:T(8,128)}, u32[]{:S(2)}, u32[]{:S(2)}) %all-to-all-start.1) | async-done | bytes 5242912 | tf_op jit(solution)/shard_map/all_to_all | solution.py:120
  312.7 4.7 %gather_fusion.3 = f32[32,16,1280]{2,1,0:T(8,128)} fusion(f32[64,16,1280]{2,1,0:T(8,128)} %all-to-all-done.1, s32[1024]{0:T(1024)S(1)} %pad_clamp_fusion), kind=kCustom, calls=%fused_computation.3 | custom fusion | bytes 5243008 | tf_op jit(solution)/shard_map/jit(_take)/gather | solution.py:121
  317.4 2.0 broadcast_select_fusion
  321.1 2.2 copy.21
  323.3 1.3 fusion.17
  325.4 6.2 %fusion = bf16[512,1024]{1,0:T(8,128)(2,1)} fusion(f32[32,16,1024]{2,1,0:T(8,128)S(1)} %slice-done, bf16[512,2048]{1,0:T(8,128)(2,1)} %all-gather.3.cloned.1.call-done, bf16[1024,2048]{1,0:T(8,128)(2,1)} %param.9), kind=kOutput, calls=%fused_computation.7 | convolution fusion | flops 2148532224 | bytes 9437184 | tf_op jit(solution)/shard_map/dot_general | solution.py:131
  (79 shorter events, 12.9 us)
Async XLA Ops:
  7.2 95.3 %copy-start = (bf16[8,1024,64]{1,2,0:T(8,128)(2,1)S(1)}, bf16[8,1024,64]{1,2,0:T(8,128)(2,1)}, u32[]{:S(2)}) copy-start(bf16[8,1024,64]{1,2,0:T(8,128)(2,1)} %param.10) | copy-start | bytes 3145732
  17.7 11.3 %copy-start.8 = (u32[256]{0:T(256)S(1)}, u32[256]{0:T(256)}, u32[]{:S(2)}) copy-start(u32[256]{0:T(256)} %constant.123) | copy-start | bytes 3076
  17.7 12.6 %copy-start.7 = (s32[32]{0:T(128)S(1)}, s32[32]{0:T(128)}, u32[]{:S(2)}) copy-start(s32[32]{0:T(128)} %param.12) | copy-start | bytes 388
  17.7 74.4 %copy-start.1 = (s32[256]{0:T(256)S(1)}, s32[256]{0:T(256)}, u32[]{:S(2)}) copy-start(s32[256]{0:T(256)} %param.13) | copy-start | bytes 3076
  17.7 82.9 %all-to-all-start = ((bf16[64,16,1280]{2,1,0:T(8,128)(2,1)}), bf16[64,16,1280]{2,1,0:T(8,128)(2,1)}, u32[]{:S(2)}, u32[]{:S(2)}) async-start(bf16[64,16,1280]{2,1,0:T(8,128)(2,1)} %select_select_fusion), calls=%async_computation.1 | async-start | bytes 5242880 | tf_op jit(solution)/shard_map/all_to_all | solution.py:56
  29.0 144.9 %all-reduce.3.cloned.1.call-start = ((), (), s32[]{:S(2)}) async-start(), calls=%async_computation.4 | async-start | bytes 1048576 | tf_op jit(solution)/shard_map/psum | solution.py:91
  103.7 2.2 copy-start.6
  105.1 0.8 copy-start.3
  107.3 216.0 %reduce-scatter.2.cloned.1.call-start = ((), (), s32[]{:S(2)}) async-start(), calls=%async_computation.3 | async-start | bytes 4718592 | tf_op jit(solution)/shard_map/reduce_scatter | solution.py:123
  114.3 0.7 copy-start.5
  173.9 2.5 copy-start.4
  180.6 132.1 %all-to-all-start.1 = ((f32[64,16,1280]{2,1,0:T(8,128)}), f32[64,16,1280]{2,1,0:T(8,128)}, u32[]{:S(2)}, u32[]{:S(2)}) async-start(f32[64,16,1280]{2,1,0:T(8,128)} %pad_maximum_fusion), calls=%async_computation.2 | async-start | bytes 10485760 | tf_op jit(solution)/shard_map/all_to_all | solution.py:120
  190.2 135.2 %all-gather.3.cloned.1.call-start = ((), (), s32[]{:S(2)}) async-start(), calls=%async_computation.5 | async-start | bytes 2359296 | tf_op jit(solution)/shard_map/all_gather | solution.py:132
  319.4 1.7 copy-start.2
  321.1 4.3 %slice-start = ((f32[32,16,1280]{2,1,0:T(8,128)}), f32[32,16,1024]{2,1,0:T(8,128)S(1)}, s32[]{:S(2)}) async-start(f32[32,16,1280]{2,1,0:T(8,128)} %copy-done.2), calls=%async_computation.6 | async-start | bytes 4194304 | tf_op jit(solution)/shard_map/slice | solution.py:141
Sparse Core Ops, SparseCore 0:
  107.4 66.4 all-reduce.2
  176.4 40.2 reduce-scatter.1
  218.6 29.6 all-gather.2

commit v2 on v1

v2 whole, which is shorter than its diff:
```python
import jax
import jax.numpy as jnp
from jax import lax
from jax.sharding import PartitionSpec as P

ALPHA = 32
BLOCK_TOKENS = 16


def route(block_slot, number_adapters, capacity):
    owner_ids = block_slot // number_adapters
    block_ids = jnp.arange(block_slot.shape[-1], dtype=jnp.int32)
    earlier = (owner_ids[..., :, None] == owner_ids[..., None, :]) & (
        block_ids[None, :] < block_ids[:, None]
    )
    position = jnp.sum(earlier.astype(jnp.int32), axis=-1)
    return owner_ids * capacity + position


def per_device(
    tokens,
    frozen_weight,
    adapter_down_matrices,
    adapter_up_matrices,
    adapter_per_block,
    slot_per_adapter,
    rank_per_adapter,
    output_gradient,
):
    tok_count = lax.axis_size("tok")
    me = lax.axis_index("tok")
    token_rows, width_portion = tokens.shape
    column_portion = output_gradient.shape[1]
    block_count = adapter_per_block.shape[0]
    number_adapters, _, rank_ceiling = adapter_down_matrices.shape
    capacity = max(2, 2 * block_count // tok_count)
    slots = tok_count * capacity
    row_total = slots * BLOCK_TOKENS
    lane = width_portion + column_portion

    block_slot = jnp.take(slot_per_adapter, adapter_per_block)
    destination = route(block_slot, number_adapters, capacity)
    local_index = block_slot % number_adapters
    slot_ids = jnp.arange(slots, dtype=jnp.int32)
    hit = destination[None, :] == slot_ids[:, None]
    filled = jnp.any(hit, axis=1)
    source_block = jnp.sum(
        jnp.where(hit, jnp.arange(block_count, dtype=jnp.int32)[None, :], 0), axis=1
    )
    tag = jnp.zeros((block_count, BLOCK_TOKENS, 128), jnp.bfloat16)
    tag = tag.at[:, 0, 0].set((local_index + 1).astype(jnp.bfloat16))
    packed = jnp.concatenate(
        [
            tokens.reshape(block_count, BLOCK_TOKENS, width_portion),
            output_gradient.reshape(block_count, BLOCK_TOKENS, column_portion),
            tag,
        ],
        axis=2,
    )
    send = jnp.where(filled[:, None, None], jnp.take(packed, source_block, axis=0), 0)
    send = send.reshape(tok_count, capacity, BLOCK_TOKENS, lane + 128)

    stored_ids = me * number_adapters + jnp.arange(number_adapters, dtype=jnp.int32)
    stored_match = slot_per_adapter[None, :] == stored_ids[:, None]
    stored_rank = jnp.sum(jnp.where(stored_match, rank_per_adapter[None, :], 0), axis=1)
    stored_scale = jnp.where(
        stored_rank > 0, jnp.float32(ALPHA) / jnp.maximum(stored_rank, 1).astype(jnp.float32), 0.0
    )
    part_rows = tok_count * BLOCK_TOKENS

    def owner_part(arrived, previous):
        slot_adapter = arrived[:, 0, lane].astype(jnp.int32) - 1
        input_rows = arrived[:, :, :width_portion].reshape(part_rows, width_portion)
        grad_rows = arrived[:, :, width_portion:lane].reshape(part_rows, column_portion)
        chosen = slot_adapter[:, None] == jnp.arange(number_adapters, dtype=jnp.int32)[None, :]
        chosen_rows = jnp.broadcast_to(
            chosen[:, None, :], (tok_count, BLOCK_TOKENS, number_adapters)
        ).reshape(part_rows, number_adapters)
        chosen_float = chosen_rows.astype(jnp.float32)
        row_rank = jnp.sum(jnp.where(chosen_rows, stored_rank[None, :], 0), axis=1)
        scale_per_row = jnp.sum(chosen_float * stored_scale[None, :], axis=1)
        keep_cols = jnp.arange(rank_ceiling, dtype=jnp.int32)[None, :] < row_rank[:, None]
        reduced_every_row = jnp.einsum(
            "ue,meb->umb", input_rows, adapter_down_matrices, preferred_element_type=jnp.float32
        )
        low_part = jnp.sum(reduced_every_row * chosen_float[:, :, None], axis=1)
        gathered_every_row = jnp.einsum(
            "hs,gbs->hgb", grad_rows, adapter_up_matrices, preferred_element_type=jnp.float32
        )
        pull_part = jnp.sum(gathered_every_row * chosen_float[:, :, None], axis=1)
        partial_sums = jnp.concatenate([low_part, pull_part], axis=1)
        if previous is not None:
            partial_sums, _ = lax.optimization_barrier((partial_sums, previous))
        both = lax.psum(partial_sums, "tp")
        low_sum = both[:, :rank_ceiling]
        pull_sum = both[:, rank_ceiling:]
        reduced_rows = jnp.where(keep_cols, low_sum, 0.0).astype(jnp.bfloat16)
        reduced_gradient = (
            scale_per_row[:, None] * jnp.where(keep_cols, pull_sum, 0.0)
        ).astype(jnp.bfloat16)
        chosen_half = chosen_rows.astype(jnp.bfloat16)
        reduced_picked = chosen_half[:, :, None] * reduced_rows[:, None, :]
        gradient_picked = chosen_half[:, :, None] * reduced_gradient[:, None, :]
        adapter_increment = scale_per_row[:, None] * jnp.einsum(
            "hnq,nqs->hs", reduced_picked, adapter_up_matrices, preferred_element_type=jnp.float32
        )
        down_add = jnp.einsum(
            "rd,rak->adk", input_rows, gradient_picked, preferred_element_type=jnp.float32
        )
        up_add = jnp.einsum(
            "rak,rc->akc", reduced_picked, grad_rows, preferred_element_type=jnp.float32
        )
        adapter_output_rows = jnp.einsum(
            "ymf,mcf->yc", gradient_picked, adapter_down_matrices, preferred_element_type=jnp.float32
        )
        back = jnp.concatenate(
            [
                adapter_output_rows.reshape(tok_count, BLOCK_TOKENS, width_portion),
                adapter_increment.reshape(tok_count, BLOCK_TOKENS, column_portion),
            ],
            axis=2,
        )
        returned = lax.all_to_all(back, "tok", split_axis=0, concat_axis=0, tiled=True)
        return returned, down_add, up_add, both

    returned_parts = []
    grad_down = None
    grad_up = None
    previous = None
    for position in range(capacity):
        arrived = lax.all_to_all(
            send[:, position], "tok", split_axis=0, concat_axis=0, tiled=True
        )
        returned, down_add, up_add, previous = owner_part(arrived, previous)
        returned_parts.append(returned)
        grad_down = down_add if grad_down is None else grad_down + down_add
        grad_up = up_add if grad_up is None else grad_up + up_add
    grad_up = stored_scale[:, None, None] * grad_up
    returned = jnp.stack(returned_parts, axis=1).reshape(slots, BLOCK_TOKENS, lane)
    mine = jnp.take(returned, destination, axis=0)

    base_out = lax.psum_scatter(
        lax.dot_general(
            frozen_weight, tokens, (((0,), (1,)), ((), ())), preferred_element_type=jnp.float32
        ),
        "tp",
        scatter_dimension=0,
        tiled=True,
    ).T
    frozen_input_gradient = lax.dot_general(
        lax.all_gather(output_gradient, "tp", axis=1, tiled=True),
        frozen_weight,
        (((1,), (1,)), ((), ())),
        preferred_element_type=jnp.float32,
    )
    projected = (
        base_out + mine[:, :, width_portion:].reshape(token_rows, column_portion)
    ).astype(jnp.bfloat16)
    token_gradient = (
        frozen_input_gradient + mine[:, :, :width_portion].reshape(token_rows, width_portion)
    ).astype(jnp.bfloat16)
    return (projected, token_gradient, grad_down, grad_up)


def solution(mesh):
    return jax.shard_map(
        per_device,
        mesh=mesh,
        in_specs=(
            P("tok", "tp"),
            P("tp", None),
            P("tok", "tp", None),
            P("tok", None, "tp"),
            P("tok"),
            P(),
            P(),
            P("tok", "tp"),
        ),
        out_specs=(P("tok", "tp"), P("tok", "tp"), P("tok", "tp", None), P("tok", None, "tp")),
        check_vma=False,
    )
```

time: 339 us -> 319 us (0.941)
  blocking collectives: 61.4 us -> 46.6 us
  other arithmetic: 16.6 us -> 27.4 us
  waiting for transfers between devices: 175 us -> 166 us
  local copies, waits for them, and re-layouts: 26.4 us -> 20.3 us
    unnamed x1 -> x0, blocking collectives: 61.4 us -> none
    all_to_all x0 -> x1, blocking collectives: none -> 46.6 us  [per_device(): lax.all_to_all(send[:, position], 'tok', split_axis=0, concat_axis=0, til...]
    all_to_all x2 -> x3, waiting for transfers between devices: 117 us -> 89.1 us  [the longest x2 61 us: owner_part(): lax.all_to_all(back, 'tok', split_axis=0, concat_axis=0, tiled=True)]
    psum x1 -> x2, waiting for transfers between devices: 57.9 us -> 76.2 us  [owner_part(): both = lax.psum(partial_sums, 'tp')]
    gather x2 -> x0, local copies, waits for them, and re-layouts: 6.9 us -> none  [per_device(): all_slot = jnp.take(slot_per_adapter, all_blocks)]
    another operation x0 -> x2, other arithmetic: none -> 5.31 us  [the longest x1 5.3 us: per_device(): jnp.stack(returned_parts, axis=1).reshape(slots, BLOCK_TOKENS, lane)]
    dot_general x5 -> x10, matrix products: 8.09 us -> 6.99 us  [the longest x2 2.76 us: owner_part(): jnp.einsum('rd,rak->adk', input_rows, gradient_picked, preferred_element_...]
    all_to_all x2 -> x3, starting transfers between devices: 20.9 us -> 21.6 us  [the longest x2 15.8 us: owner_part(): lax.all_to_all(back, 'tok', split_axis=0, concat_axis=0, tiled=True)]
  transfers between devices with their start and end apart: 5 -> 7, of which waited for: 2 -> 5; matrix products, arithmetic and copies ran while one was open for 12% -> 17% of each run, Pallas kernels for 0% -> 0%
where the time goes in v2:
time: 319 us; the launch traced here: 318 us
  waiting for transfers between devices  166 us (52%)
  blocking collectives  46.6 us (15%)
  other arithmetic  27.4 us (9%)
  starting transfers between devices  21.9 us (7%)
  matrix products  21.3 us (7%)
  local copies, waits for them, and re-layouts  20.3 us (6%)
  between operations  14.3 us (4%)
    psum x2, waiting for transfers between devices, owner_part(): both = lax.psum(partial_sums, 'tp')  76.2 us
    all_to_all x2, waiting for transfers between devices, owner_part(): lax.all_to_all(back, 'tok', split_axis=0, concat_axis=0, tiled=True)  61 us
    all_to_all x1, blocking collectives, per_device(): lax.all_to_all(send[:, position], 'tok', split_axis=0, concat_axis=0, til...  46.6 us
    all_to_all x1, waiting for transfers between devices, per_device(): lax.all_to_all(send[:, position], 'tok', split_axis=0, concat_axis=0, til...  28.1 us
    all_to_all x2, starting transfers between devices, owner_part(): lax.all_to_all(back, 'tok', split_axis=0, concat_axis=0, tiled=True)  15.8 us
    dot_general x1, matrix products, per_device(): lax.dot_general(frozen_weight, tokens, (((0,), (1,)), ((), ())), preferre...  6.6 us
  transfers between devices with their start and end apart: 7, of which 5 were waited for; matrix products, arithmetic and copies ran while one was open for 17% of the time, Pallas kernels for 0%

profile of v2, /device:TPU:27, one launch (start us, length us, event | category | flops | bytes accessed | tf_op | source)
XLA Modules:
  0.0 317.9 jit_solution(7603902281128855879)
XLA Ops:
  7.9 1.4 gather_fusion
  11.3 1.4 fusion.2
  12.8 2.4 gather_fusion.1
  15.2 2.3 select_select_fusion
  17.5 1.3 slice_bitcast_fusion.1
  18.8 46.6 %all_to_all.20 = bf16[32,16,1408]{2,1,0:T(8,128)(2,1)} all-to-all(bf16[32,16,1408]{2,1,0:T(8,128)(2,1)S(1)} %get-tuple-element.42), channel_id=1, replica_groups=mesh['tok'=32,'tp'=8] {'tok'}, dimensions={0} | all-to-all | bytes 2883584 | tf_op jit(solution)/shard_map/all_to_all | solution.py:131
  65.4 5.8 %all-to-all-start.2 = ((bf16[32,16,1408]{2,1,0:T(8,128)(2,1)}), bf16[32,16,1408]{2,1,0:T(8,128)(2,1)S(1)}, u32[]{:S(2)}, u32[]{:S(2)}) async-start(bf16[32,16,1408]{2,1,0:T(8,128)(2,1)} %get-tuple-element.43), calls=%async_computation.3 | async-start | bytes 2883584 | tf_op jit(solution)/shard_map/all_to_all | solution.py:131
  71.2 1.5 fusion.46
  78.0 28.1 %all-to-all-done.2 = bf16[32,16,1408]{2,1,0:T(8,128)(2,1)S(1)} async-done(((bf16[32,16,1408]{2,1,0:T(8,128)(2,1)}), bf16[32,16,1408]{2,1,0:T(8,128)(2,1)S(1)}, u32[]{:S(2)}, u32[]{:S(2)}) %all-to-all-start.2) | async-done | bytes 1441824 | tf_op jit(solution)/shard_map/all_to_all | solution.py:131
  108.1 1.6 convert_element_type.111
  112.5 32.1 %all-reduce.4.cloned.1.call-done = f32[512,128]{0,1:T(8,128)} async-done(((f32[512,128]{0,1:T(8,128)}), f32[512,128]{0,1:T(8,128)}) %all-reduce.4.cloned.1.call-update) | async-done | bytes 262160 | tf_op jit(solution)/shard_map/psum | solution.py:94
  150.0 1.7 pad_maximum_fusion.1
  151.8 9.8 %all-to-all-start.1 = ((f32[32,16,1280]{2,1,0:T(8,128)}), f32[32,16,1280]{2,1,0:T(8,128)}, u32[]{:S(2)}, u32[]{:S(2)}) async-start(f32[32,16,1280]{2,1,0:T(8,128)} %pad_maximum_fusion.1), calls=%async_computation.2 | async-start | bytes 5242880 | tf_op jit(solution)/shard_map/all_to_all | solution.py:123
  161.8 6.6 %fusion.57 = f32[2048,512]{1,0:T(8,128)} fusion(bf16[1024,2048]{1,0:T(8,128)(2,1)} %param.11, bf16[512,1024]{1,0:T(8,128)(2,1)S(1)} %copy-done.7), kind=kOutput, calls=%fused_computation.117 | convolution fusion | flops 2147483648 | bytes 9437184 | tf_op jit(solution)/shard_map/dot_general | solution.py:143
  169.5 44.1 %all-reduce.6.cloned.1.call-done = f32[512,128]{0,1:T(8,128)} async-done(((f32[512,128]{0,1:T(8,128)}), f32[512,128]{0,1:T(8,128)}) %all-reduce.6.cloned.1.call-update) | async-done | bytes 262160 | tf_op jit(solution)/shard_map/psum | solution.py:94
  216.6 1.8 pad_maximum_fusion.2
  218.3 4.4 %all-to-all-done.1 = f32[32,16,1280]{2,1,0:T(8,128)} async-done(((f32[32,16,1280]{2,1,0:T(8,128)}), f32[32,16,1280]{2,1,0:T(8,128)}, u32[]{:S(2)}, u32[]{:S(2)}) %all-to-all-start.1) | async-done | bytes 2621472 | tf_op jit(solution)/shard_map/all_to_all | solution.py:123
  222.8 6.1 %all-to-all-start.3 = ((f32[32,16,1280]{2,1,0:T(8,128)}), f32[32,16,1280]{2,1,0:T(8,128)}, u32[]{:S(2)}, u32[]{:S(2)}) async-start(f32[32,16,1280]{2,1,0:T(8,128)} %pad_maximum_fusion.2), calls=%async_computation.4 | async-start | bytes 5242880 | tf_op jit(solution)/shard_map/all_to_all | solution.py:123
  231.1 2.0 add_bitcast_fusion
  233.1 56.5 %all-to-all-done.3 = f32[32,16,1280]{2,1,0:T(8,128)} async-done(((f32[32,16,1280]{2,1,0:T(8,128)}), f32[32,16,1280]{2,1,0:T(8,128)}, u32[]{:S(2)}, u32[]{:S(2)}) %all-to-all-start.3) | async-done | bytes 2621472 | tf_op jit(solution)/shard_map/all_to_all | solution.py:123
  289.7 5.3 %pad_maximum_fusion = f32[32,2,16,1280]{3,2,1,0:T(8,128)} fusion(f32[32,1,16,1280]{3,2,1,0:T(8,128)} %bitcast.30, f32[32,1,16,1280]{3,2,1,0:T(8,128)} %bitcast.18), kind=kLoop, calls=%fused_computation.3 | loop fusion | flops 1310720 | bytes 10485760 | tf_op jit(solution)/shard_map/stack | solution.py:139
  295.0 4.7 %gather_fusion.2 = f32[32,16,1280]{2,1,0:T(8,128)} fusion(f32[64,16,1280]{2,1,0:T(8,128)} %bitcast.94, s32[1024]{0:T(1024)S(1)} %pad_clamp_fusion), kind=kCustom, calls=%fused_computation.2 | custom fusion | bytes 5243008 | tf_op jit(solution)/shard_map/jit(_take)/gather | solution.py:140
  299.6 2.0 broadcast_select_fusion
  303.0 6.2 %fusion.1 = bf16[512,1024]{1,0:T(8,128)(2,1)} fusion(f32[32,16,1024]{2,1,0:T(8,128)S(1)} %slice.94, bf16[512,2048]{1,0:T(8,128)(2,1)} %all-gather.2.cloned.1.call-done, bf16[1024,2048]{1,0:T(8,128)(2,1)} %param.11), kind=kOutput, calls=%fused_computation.10 | convolution fusion | flops 2148532224 | bytes 9437184 | tf_op jit(solution)/shard_map/dot_general | solution.py:150
  (129 shorter events, 27.8 us)
Async XLA Ops:
  7.2 68.8 %copy-start = (bf16[8,1024,64]{1,2,0:T(8,128)(2,1)S(1)}, bf16[8,1024,64]{1,2,0:T(8,128)(2,1)}, u32[]{:S(2)}) copy-start(bf16[8,1024,64]{1,2,0:T(8,128)(2,1)} %param.12) | copy-start | bytes 3145732
  65.4 40.6 %all-to-all-start.2 = ((bf16[32,16,1408]{2,1,0:T(8,128)(2,1)}), bf16[32,16,1408]{2,1,0:T(8,128)(2,1)S(1)}, u32[]{:S(2)}, u32[]{:S(2)}) async-start(bf16[32,16,1408]{2,1,0:T(8,128)(2,1)} %get-tuple-element.43), calls=%async_computation.3 | async-start | bytes 2883584 | tf_op jit(solution)/shard_map/all_to_all | solution.py:131
  71.2 73.5 %all-reduce.4.cloned.1.call-start = ((), (), s32[]{:S(2)}) async-start(), calls=%async_computation.6 | async-start | bytes 524288 | tf_op jit(solution)/shard_map/psum | solution.py:94
  73.6 3.1 copy-start.10
  74.9 1.9 copy-start.22
  77.9 135.7 %all-reduce.6.cloned.1.call-start = ((), (), s32[]{:S(2)}) async-start(), calls=%async_computation.7 | async-start | bytes 524288 | tf_op jit(solution)/shard_map/psum | solution.py:94
  107.3 38.3 %copy-start.14 = (pred[32,8]{0,1:T(8,128)(4,1)}, pred[32,8]{0,1:T(8,128)(4,1)S(1)}, u32[]{:S(2)}) copy-start(pred[32,8]{0,1:T(8,128)(4,1)S(1)} %get-tuple-element.49) | copy-start | bytes 772
  109.8 2.0 copy-start.3
  110.6 34.8 %copy-start.2 = (s32[256]{0:T(256)S(1)}, s32[256]{0:T(256)}, u32[]{:S(2)}) copy-start(s32[256]{0:T(256)} %param.15) | copy-start | bytes 3076
  110.6 34.8 %copy-start.19 = (s32[256]{0:T(256)S(1)}, s32[256]{0:T(256)}, u32[]{:S(2)}) copy-start(s32[256]{0:T(256)} %param.16) | copy-start | bytes 3076
  144.7 158.3 %all-gather.2.cloned.1.call-start = ((), (), s32[]{:S(2)}) async-start(), calls=%async_computation.8 | async-start | bytes 2359296 | tf_op jit(solution)/shard_map/all_gather | solution.py:151
  145.6 3.1 copy-start.16
  149.7 2.1 copy-start.12
  151.8 10.0 %copy-start.7 = (bf16[512,1024]{1,0:T(8,128)(2,1)S(1)}, bf16[512,1024]{1,0:T(8,128)(2,1)}, u32[]{:S(2)}) copy-start(bf16[512,1024]{1,0:T(8,128)(2,1)} %param.10) | copy-start | bytes 3145732
  151.8 71.0 %all-to-all-start.1 = ((f32[32,16,1280]{2,1,0:T(8,128)}), f32[32,16,1280]{2,1,0:T(8,128)}, u32[]{:S(2)}, u32[]{:S(2)}) async-start(f32[32,16,1280]{2,1,0:T(8,128)} %pad_maximum_fusion.1), calls=%async_computation.2 | async-start | bytes 5242880 | tf_op jit(solution)/shard_map/all_to_all | solution.py:123
  161.6 147.7 %reduce-scatter.2.cloned.1.call-start = ((), (), s32[]{:S(2)}) async-start(), calls=%async_computation.5 | async-start | bytes 4718592 | tf_op jit(solution)/shard_map/reduce_scatter | solution.py:142
  168.4 47.0 %copy-start.25 = (bf16[8,64,256]{2,1,0:T(8,128)(2,1)S(1)}, bf16[8,64,256]{2,1,0:T(8,128)(2,1)}, u32[]{:S(2)}) copy-start(bf16[8,64,256]{2,1,0:T(8,128)(2,1)} %param.13) | copy-start | bytes 786436
  218.3 10.5 %copy-start.21 = (s32[32]{0:T(128)S(1)}, s32[32]{0:T(128)}, u32[]{:S(2)}) copy-start(s32[32]{0:T(128)} %copy-done.20) | copy-start | bytes 388
  218.3 10.6 %copy-start.9 = (bf16[32,16,256]{2,1,0:T(8,128)(2,1)S(1)}, bf16[32,16,256]{2,1,0:T(8,128)(2,1)}, u32[]{:S(2)}) copy-start(bf16[32,16,256]{2,1,0:T(8,128)(2,1)} %copy-done.8) | copy-start | bytes 786436
  218.3 10.6 %copy-start.13 = (bf16[512,64]{0,1:T(8,128)(2,1)S(1)}, bf16[512,64]{0,1:T(8,128)(2,1)}, u32[]{:S(2)}) copy-start(bf16[512,64]{0,1:T(8,128)(2,1)} %copy-done.12) | copy-start | bytes 196612
  222.8 66.9 %all-to-all-start.3 = ((f32[32,16,1280]{2,1,0:T(8,128)}), f32[32,16,1280]{2,1,0:T(8,128)}, u32[]{:S(2)}, u32[]{:S(2)}) async-start(f32[32,16,1280]{2,1,0:T(8,128)} %pad_maximum_fusion.2), calls=%async_computation.4 | async-start | bytes 5242880 | tf_op jit(solution)/shard_map/all_to_all | solution.py:123
  228.9 2.2 copy-start.4
  295.0 4.7 %copy-start.18 = (pred[32]{0:T(512)(128)(4,1)S(1)}, pred[32]{0:T(512)(128)(4,1)}, u32[]{:S(2)}) copy-start(pred[32]{0:T(512)(128)(4,1)} %get-tuple-element.38) | copy-start | bytes 100
  303.0 8.4 %copy-start.1 = (bf16[8,1024,64]{1,2,0:T(8,128)(2,1)S(1)}, bf16[8,1024,64]{1,2,0:T(8,128)(2,1)}, u32[]{:S(2)}) copy-start(bf16[8,1024,64]{1,2,0:T(8,128)(2,1)} %param.12) | copy-start | bytes 3145732
  (9 other events, 10.4 us)
Sparse Core Ops, SparseCore 0:
  78.0 66.5 all-reduce.3
  147.5 66.0 all-reduce.5
  215.4 29.5 all-gather.1
  247.5 40.8 reduce-scatter.1

commit v3 on v2

--- a/solution.py
+++ b/solution.py
@@ -15,6 +15,16 @@
     )
     position = jnp.sum(earlier.astype(jnp.int32), axis=-1)
     return owner_ids * capacity + position
+
+
+def tree_sum(value, axis):
+    size = lax.axis_size(axis)
+    step = 1
+    while step < size:
+        pairs = [(i, i ^ step) for i in range(size)]
+        value = value + lax.ppermute(value, axis, pairs)
+        step *= 2
+    return value
 
 
 def per_device(
@@ -91,7 +101,7 @@
         partial_sums = jnp.concatenate([low_part, pull_part], axis=1)
         if previous is not None:
             partial_sums, _ = lax.optimization_barrier((partial_sums, previous))
-        both = lax.psum(partial_sums, "tp")
+        both = tree_sum(partial_sums, "tp")
         low_sum = both[:, :rank_ceiling]
         pull_sum = both[:, rank_ceiling:]
         reduced_rows = jnp.where(keep_cols, low_sum, 0.0).astype(jnp.bfloat16)

time: 319 us -> 289 us (0.906); the launches traced: 318 us -> 285 us
  waiting for transfers between devices: 166 us -> 118 us
  local copies, waits for them, and re-layouts: 20.3 us -> 27.5 us
  starting transfers between devices: 21.9 us -> 26.2 us
  other arithmetic: 27.4 us -> 31.3 us
    psum x2 -> x0, waiting for transfers between devices: 76.2 us -> none  [owner_part(): both = lax.psum(partial_sums, 'tp')]
    all_to_all x2, waiting for transfers between devices: 61 us -> 85.5 us  [owner_part(): lax.all_to_all(back, 'tok', split_axis=0, concat_axis=0, tiled=True)]
    ppermute x0 -> x6, waiting for transfers between devices: none -> 14.8 us  [tree_sum(): value = value + lax.ppermute(value, axis, pairs)]
    all_to_all x1, waiting for transfers between devices: 28.1 us -> 17.2 us  [per_device(): lax.all_to_all(send[:, position], 'tok', split_axis=0, concat_axis=0, til...]
    ppermute x0 -> x6, starting transfers between devices: none -> 8.39 us  [tree_sum(): value = value + lax.ppermute(value, axis, pairs)]
    add x0 -> x6, other arithmetic: none -> 4.75 us  [tree_sum(): value = value + lax.ppermute(value, axis, pairs)]
    all_to_all x2, starting transfers between devices: 15.8 us -> 12 us  [owner_part(): lax.all_to_all(back, 'tok', split_axis=0, concat_axis=0, tiled=True)]
  transfers between devices with their start and end apart: 7 -> 11, of which waited for: 5 -> 6; matrix products, arithmetic and copies ran while one was open for 17% -> 20% of each run, Pallas kernels for 0% -> 0%
where the time goes in v3:
time: 289 us; the launch traced here: 285 us
  waiting for transfers between devices  118 us (41%)
  blocking collectives  46.6 us (16%)
  other arithmetic  31.3 us (11%)
  local copies, waits for them, and re-layouts  27.5 us (10%)
  starting transfers between devices  26.2 us (9%)
  matrix products  20.2 us (7%)
  between operations  14.7 us (5%)
    all_to_all x2, waiting for transfers between devices, owner_part(): lax.all_to_all(back, 'tok', split_axis=0, concat_axis=0, tiled=True)  85.5 us
    all_to_all x1, blocking collectives, per_device(): lax.all_to_all(send[:, position], 'tok', split_axis=0, concat_axis=0, til...  46.6 us
    all_to_all x1, waiting for transfers between devices, per_device(): lax.all_to_all(send[:, position], 'tok', split_axis=0, concat_axis=0, til...  17.2 us
    ppermute x6, waiting for transfers between devices, tree_sum(): value = value + lax.ppermute(value, axis, pairs)  14.8 us
    all_to_all x2, starting transfers between devices, owner_part(): lax.all_to_all(back, 'tok', split_axis=0, concat_axis=0, tiled=True)  12 us
    ppermute x6, starting transfers between devices, tree_sum(): value = value + lax.ppermute(value, axis, pairs)  8.39 us
    dot_general x1, matrix products, per_device(): lax.dot_general(lax.all_gather(output_gradient, 'tp', axis=1, tiled=True)...  6.25 us
  transfers between devices with their start and end apart: 11, of which 6 were waited for; matrix products, arithmetic and copies ran while one was open for 20% of the time, Pallas kernels for 0%

profile of v3, /device:TPU:27, one launch (start us, length us, event | category | flops | bytes accessed | tf_op | source)
XLA Modules:
  0.0 284.6 jit_solution(12579409214109218701)
XLA Ops:
  12.7 2.4 gather_fusion.1
  15.2 2.3 select_select_fusion
  18.8 46.6 %all_to_all.20 = bf16[32,16,1408]{2,1,0:T(8,128)(2,1)} all-to-all(bf16[32,16,1408]{2,1,0:T(8,128)(2,1)S(1)} %get-tuple-element.42), channel_id=1, replica_groups=mesh['tok'=32,'tp'=8] {'tok'}, dimensions={0} | all-to-all | bytes 2883584 | tf_op jit(solution)/shard_map/all_to_all | solution.py:141
  65.4 5.8 %all-to-all-start.2 = ((bf16[32,16,1408]{2,1,0:T(8,128)(2,1)}), bf16[32,16,1408]{2,1,0:T(8,128)(2,1)S(1)}, u32[]{:S(2)}, u32[]{:S(2)}) async-start(bf16[32,16,1408]{2,1,0:T(8,128)(2,1)} %get-tuple-element.43), calls=%async_computation.3 | async-start | bytes 2883584 | tf_op jit(solution)/shard_map/all_to_all | solution.py:141
  78.8 1.9 collective-permute-start
  80.7 4.5 %fusion.58 = f32[2048,512]{1,0:T(8,128)} fusion(bf16[1024,2048]{1,0:T(8,128)(2,1)S(1)} %copy-done.30, bf16[512,1024]{1,0:T(8,128)(2,1)S(1)} %copy-done.9), kind=kOutput, calls=%fused_computation.118 | convolution fusion | flops 2147483648 | bytes 9437184 | tf_op jit(solution)/shard_map/dot_general | solution.py:153
  86.1 1.8 fusion.57
  88.9 17.2 %all-to-all-done.2 = bf16[32,16,1408]{2,1,0:T(8,128)(2,1)S(1)} async-done(((bf16[32,16,1408]{2,1,0:T(8,128)(2,1)}), bf16[32,16,1408]{2,1,0:T(8,128)(2,1)S(1)}, u32[]{:S(2)}, u32[]{:S(2)}) %all-to-all-start.2) | async-done | bytes 1441824 | tf_op jit(solution)/shard_map/all_to_all | solution.py:141
  106.7 1.8 add.144
  123.1 1.7 pad_maximum_fusion.1
  124.8 6.4 %all-to-all-start.1 = ((f32[32,16,1280]{2,1,0:T(8,128)}), f32[32,16,1280]{2,1,0:T(8,128)}, u32[]{:S(2)}, u32[]{:S(2)}) async-start(f32[32,16,1280]{2,1,0:T(8,128)} %pad_maximum_fusion.1), calls=%async_computation.2 | async-start | bytes 5242880 | tf_op jit(solution)/shard_map/all_to_all | solution.py:133
  132.0 1.6 convert_element_type.111
  135.2 3.1 %collective-permute-start.3 = (f32[512,128]{0,1:T(8,128)S(1)}, f32[512,128]{0,1:T(8,128)S(1)}, u32[]{:S(2)}, u32[]{:S(2)}) collective-permute-start(f32[512,128]{0,1:T(8,128)S(1)} %pad_maximum_fusion.4), channel_id=1, source_target_pairs={{0,1},{1,0},{2,3},{3,2},{4,5},{5,4},{6,7},{7,6},{8,9},{9,8},{10,11... | collective-permute-start | bytes 786440 | tf_op jit(solution)/shard_map/ppermute | solution.py:25
  140.1 7.2 %collective-permute-done.4 = f32[512,128]{0,1:T(8,128)S(1)} collective-permute-done((f32[512,128]{0,1:T(8,128)S(1)}, f32[512,128]{0,1:T(8,128)S(1)}, u32[]{:S(2)}, u32[]{:S(2)}) %collective-permute-start.4) | collective-permute-done | bytes 262176 | tf_op jit(solution)/shard_map/ppermute | solution.py:25
  149.2 6.4 %collective-permute-done.5 = f32[512,128]{0,1:T(8,128)S(1)} collective-permute-done((f32[512,128]{0,1:T(8,128)S(1)}, f32[512,128]{0,1:T(8,128)S(1)}, u32[]{:S(2)}, u32[]{:S(2)}) %collective-permute-start.5) | collective-permute-done | bytes 262176 | tf_op jit(solution)/shard_map/ppermute | solution.py:25
  157.8 1.8 pad_maximum_fusion.2
  159.6 31.2 %all-to-all-done.1 = f32[32,16,1280]{2,1,0:T(8,128)} async-done(((f32[32,16,1280]{2,1,0:T(8,128)}), f32[32,16,1280]{2,1,0:T(8,128)}, u32[]{:S(2)}, u32[]{:S(2)}) %all-to-all-start.1) | async-done | bytes 2621472 | tf_op jit(solution)/shard_map/all_to_all | solution.py:133
  190.7 5.6 %all-to-all-start.3 = ((f32[32,16,1280]{2,1,0:T(8,128)}), f32[32,16,1280]{2,1,0:T(8,128)}, u32[]{:S(2)}, u32[]{:S(2)}) async-start(f32[32,16,1280]{2,1,0:T(8,128)} %pad_maximum_fusion.2), calls=%async_computation.4 | async-start | bytes 5242880 | tf_op jit(solution)/shard_map/all_to_all | solution.py:133
  199.3 2.0 add_bitcast_fusion
  201.3 54.4 %all-to-all-done.3 = f32[32,16,1280]{2,1,0:T(8,128)} async-done(((f32[32,16,1280]{2,1,0:T(8,128)}), f32[32,16,1280]{2,1,0:T(8,128)}, u32[]{:S(2)}, u32[]{:S(2)}) %all-to-all-start.3) | async-done | bytes 2621472 | tf_op jit(solution)/shard_map/all_to_all | solution.py:133
  255.7 5.3 %pad_maximum_fusion = f32[32,2,16,1280]{3,2,1,0:T(8,128)} fusion(f32[32,1,16,1280]{3,2,1,0:T(8,128)} %bitcast.30, f32[32,1,16,1280]{3,2,1,0:T(8,128)} %bitcast.18), kind=kLoop, calls=%fused_computation.3 | loop fusion | flops 1310720 | bytes 10485760 | tf_op jit(solution)/shard_map/stack | solution.py:149
  261.0 4.7 %gather_fusion.2 = f32[32,16,1280]{2,1,0:T(8,128)} fusion(f32[64,16,1280]{2,1,0:T(8,128)} %bitcast.94, s32[1024]{0:T(1024)S(1)} %pad_clamp_fusion), kind=kCustom, calls=%fused_computation.2 | custom fusion | bytes 5243008 | tf_op jit(solution)/shard_map/jit(_take)/gather | solution.py:150
  265.7 2.0 broadcast_select_fusion
  271.5 6.3 %fusion.1 = bf16[512,1024]{1,0:T(8,128)(2,1)} fusion(f32[32,16,1024]{2,1,0:T(8,128)S(1)} %slice-done, bf16[512,2048]{1,0:T(8,128)(2,1)} %all-gather.2.cloned.1.call-done, bf16[1024,2048]{1,0:T(8,128)(2,1)} %param.11), kind=kOutput, calls=%fused_computation.10 | convolution fusion | flops 2148532224 | bytes 9437184 | tf_op jit(solution)/shard_map/dot_general | solution.py:160
  (158 shorter events, 46.2 us)
Async XLA Ops:
  7.2 69.3 %copy-start = (bf16[8,1024,64]{1,2,0:T(8,128)(2,1)S(1)}, bf16[8,1024,64]{1,2,0:T(8,128)(2,1)}, u32[]{:S(2)}) copy-start(bf16[8,1024,64]{1,2,0:T(8,128)(2,1)} %param.12) | copy-start | bytes 3145732
  65.4 40.6 %all-to-all-start.2 = ((bf16[32,16,1408]{2,1,0:T(8,128)(2,1)}), bf16[32,16,1408]{2,1,0:T(8,128)(2,1)S(1)}, u32[]{:S(2)}, u32[]{:S(2)}) async-start(bf16[32,16,1408]{2,1,0:T(8,128)(2,1)} %get-tuple-element.43), calls=%async_computation.3 | async-start | bytes 2883584 | tf_op jit(solution)/shard_map/all_to_all | solution.py:141
  71.1 198.3 %reduce-scatter.2.cloned.1.call-start = ((), (), s32[]{:S(2)}) async-start(), calls=%async_computation.5 | async-start | bytes 4718592 | tf_op jit(solution)/shard_map/reduce_scatter | solution.py:152
  74.1 3.1 %copy-start.15 = (f32[512,8]{0,1:T(8,128)S(1)}, f32[512,8]{0,1:T(8,128)}, u32[]{:S(2)}) copy-start(f32[512,8]{0,1:T(8,128)} %convert_element_type.104) | copy-start | bytes 49156
  76.5 4.2 %copy-start.9 = (bf16[512,1024]{1,0:T(8,128)(2,1)S(1)}, bf16[512,1024]{1,0:T(8,128)(2,1)}, u32[]{:S(2)}) copy-start(bf16[512,1024]{1,0:T(8,128)(2,1)} %param.10) | copy-start | bytes 3145732
  76.5 4.2 %copy-start.30 = (bf16[1024,2048]{1,0:T(8,128)(2,1)S(1)}, bf16[1024,2048]{1,0:T(8,128)(2,1)}, u32[]{:S(2)}) copy-start(bf16[1024,2048]{1,0:T(8,128)(2,1)} %param.11) | copy-start | bytes 12582916
  78.8 7.3 %collective-permute-start = (f32[512,128]{0,1:T(8,128)}, f32[512,128]{0,1:T(8,128)}, u32[]{:S(2)}, u32[]{:S(2)}) collective-permute-start(f32[512,128]{0,1:T(8,128)} %pad_maximum_fusion.3), channel_id=1, source_target_pairs={{0,1},{1,0},{2,3},{3,2},{4,5},{5,4},{6,7},{7,6},{8,9},{9,8},{10,11... | collective-permute-start | bytes 786440 | tf_op jit(solution)/shard_map/ppermute | solution.py:25
  87.9 18.8 %collective-permute-start.1 = (f32[512,128]{0,1:T(8,128)}, f32[512,128]{0,1:T(8,128)}, u32[]{:S(2)}, u32[]{:S(2)}) collective-permute-start(f32[512,128]{0,1:T(8,128)} %fusion.57), channel_id=1, source_target_pairs={{0,2},{1,3},{2,0},{3,1},{4,6},{5,7},{6,4},{7,5},{8,10},{9,11},{10,... | collective-permute-start | bytes 786440 | tf_op jit(solution)/shard_map/ppermute | solution.py:25
  108.5 11.4 %collective-permute-start.2 = (f32[512,128]{0,1:T(8,128)}, f32[512,128]{0,1:T(8,128)}, u32[]{:S(2)}, u32[]{:S(2)}) collective-permute-start(f32[512,128]{0,1:T(8,128)} %add.144), channel_id=1, source_target_pairs={{0,4},{1,5},{2,6},{3,7},{4,0},{5,1},{6,2},{7,3},{8,12},{9,13},{10,... | collective-permute-start | bytes 786440 | tf_op jit(solution)/shard_map/ppermute | solution.py:25
  124.8 65.9 %all-to-all-start.1 = ((f32[32,16,1280]{2,1,0:T(8,128)}), f32[32,16,1280]{2,1,0:T(8,128)}, u32[]{:S(2)}, u32[]{:S(2)}) async-start(f32[32,16,1280]{2,1,0:T(8,128)} %pad_maximum_fusion.1), calls=%async_computation.2 | async-start | bytes 5242880 | tf_op jit(solution)/shard_map/all_to_all | solution.py:133
  134.5 14.2 %copy-start.19 = (s32[32,16]{0,1:T(8,128)S(1)}, s32[32,16]{0,1:T(8,128)}, u32[]{:S(2)}) copy-start(s32[32,16]{0,1:T(8,128)} %get-tuple-element.37) | copy-start | bytes 6148
  134.5 14.3 %copy-start.23 = (bf16[32,8]{0,1:T(8,128)(2,1)S(1)}, bf16[32,8]{0,1:T(8,128)(2,1)}, u32[]{:S(2)}) copy-start(bf16[32,8]{0,1:T(8,128)(2,1)} %get-tuple-element.47) | copy-start | bytes 1540
  134.5 14.6 %copy-start.20 = (f32[32,16]{0,1:T(8,128)S(1)}, f32[32,16]{0,1:T(8,128)}, u32[]{:S(2)}) copy-start(f32[32,16]{0,1:T(8,128)} %get-tuple-element.35) | copy-start | bytes 6148
  135.2 4.3 %collective-permute-start.3 = (f32[512,128]{0,1:T(8,128)S(1)}, f32[512,128]{0,1:T(8,128)S(1)}, u32[]{:S(2)}, u32[]{:S(2)}) collective-permute-start(f32[512,128]{0,1:T(8,128)S(1)} %pad_maximum_fusion.4), channel_id=1, source_target_pairs={{0,1},{1,0},{2,3},{3,2},{4,5},{5,4},{6,7},{7,6},{8,9},{9,8},{10,11... | collective-permute-start | bytes 786440 | tf_op jit(solution)/shard_map/ppermute | solution.py:25
  139.5 7.7 %collective-permute-start.4 = (f32[512,128]{0,1:T(8,128)S(1)}, f32[512,128]{0,1:T(8,128)S(1)}, u32[]{:S(2)}, u32[]{:S(2)}) collective-permute-start(f32[512,128]{0,1:T(8,128)S(1)} %add.146), channel_id=1, source_target_pairs={{0,2},{1,3},{2,0},{3,1},{4,6},{5,7},{6,4},{7,5},{8,10},{9,11},{10,... | collective-permute-start | bytes 786440 | tf_op jit(solution)/shard_map/ppermute | solution.py:25
  147.2 8.4 %collective-permute-start.5 = (f32[512,128]{0,1:T(8,128)S(1)}, f32[512,128]{0,1:T(8,128)S(1)}, u32[]{:S(2)}, u32[]{:S(2)}) collective-permute-start(f32[512,128]{0,1:T(8,128)S(1)} %add.147), channel_id=1, source_target_pairs={{0,4},{1,5},{2,6},{3,7},{4,0},{5,1},{6,2},{7,3},{8,12},{9,13},{10,... | collective-permute-start | bytes 786440 | tf_op jit(solution)/shard_map/ppermute | solution.py:25
  159.6 37.5 %copy-start.29 = (s32[32]{0:T(128)S(1)}, s32[32]{0:T(128)}, u32[]{:S(2)}) copy-start(s32[32]{0:T(128)} %copy-done.28) | copy-start | bytes 388
  159.6 37.5 %copy-start.14 = (bf16[32,16,256]{2,1,0:T(8,128)(2,1)S(1)}, bf16[32,16,256]{2,1,0:T(8,128)(2,1)}, u32[]{:S(2)}) copy-start(bf16[32,16,256]{2,1,0:T(8,128)(2,1)} %copy-done.13) | copy-start | bytes 786436
  159.6 37.5 %copy-start.18 = (bf16[512,64]{0,1:T(8,128)(2,1)S(1)}, bf16[512,64]{0,1:T(8,128)(2,1)}, u32[]{:S(2)}) copy-start(bf16[512,64]{0,1:T(8,128)(2,1)} %copy-done.17) | copy-start | bytes 196612
  159.6 37.9 %copy-start.12 = (bf16[512,64]{0,1:T(8,128)(2,1)S(1)}, bf16[512,64]{0,1:T(8,128)(2,1)}, u32[]{:S(2)}) copy-start(bf16[512,64]{0,1:T(8,128)(2,1)} %copy-done.11) | copy-start | bytes 196612
  190.7 65.0 %all-to-all-start.3 = ((f32[32,16,1280]{2,1,0:T(8,128)}), f32[32,16,1280]{2,1,0:T(8,128)}, u32[]{:S(2)}, u32[]{:S(2)}) async-start(f32[32,16,1280]{2,1,0:T(8,128)} %pad_maximum_fusion.2), calls=%async_computation.4 | async-start | bytes 5242880 | tf_op jit(solution)/shard_map/all_to_all | solution.py:133
  196.3 75.2 %all-gather.2.cloned.1.call-start = ((), (), s32[]{:S(2)}) async-start(), calls=%async_computation.6 | async-start | bytes 2359296 | tf_op jit(solution)/shard_map/all_gather | solution.py:161
  261.0 4.7 %copy-start.26 = (pred[32]{0:T(512)(128)(4,1)S(1)}, pred[32]{0:T(512)(128)(4,1)}, u32[]{:S(2)}) copy-start(pred[32]{0:T(512)(128)(4,1)} %get-tuple-element.38) | copy-start | bytes 100
  271.5 6.3 %copy-start.1 = (bf16[8,1024,64]{1,2,0:T(8,128)(2,1)S(1)}, bf16[8,1024,64]{1,2,0:T(8,128)(2,1)}, u32[]{:S(2)}) copy-start(bf16[8,1024,64]{1,2,0:T(8,128)(2,1)} %param.12) | copy-start | bytes 3145732
  (22 other events, 28.2 us)
Sparse Core Ops, SparseCore 0:
  85.4 45.2 reduce-scatter.1
  199.0 32.8 all-gather.1

commit v4 on v3

--- a/solution.py
+++ b/solution.py
@@ -23,6 +23,24 @@
     while step < size:
         pairs = [(i, i ^ step) for i in range(size)]
         value = value + lax.ppermute(value, axis, pairs)
+        step *= 2
+    return value
+
+
+def tree_gather(value, axis):
+    size = lax.axis_size(axis)
+    me = lax.axis_index(axis)
+    value = value[None]
+    step = 1
+    while step < size:
+        pairs = [(i, i ^ step) for i in range(size)]
+        other = lax.ppermute(value, axis, pairs)
+        low_side = (me & step) == 0
+        value = jnp.where(
+            low_side,
+            jnp.concatenate([value, other], axis=0),
+            jnp.concatenate([other, value], axis=0),
+        )
         step *= 2
     return value
 
@@ -38,6 +56,7 @@
     output_gradient,
 ):
     tok_count = lax.axis_size("tok")
+    tp_count = lax.axis_size("tp")
     me = lax.axis_index("tok")
     token_rows, width_portion = tokens.shape
     column_portion = output_gradient.shape[1]
@@ -123,10 +142,23 @@
         adapter_output_rows = jnp.einsum(
             "ymf,mcf->yc", gradient_picked, adapter_down_matrices, preferred_element_type=jnp.float32
         )
+        every_column = tree_gather(grad_rows, "tp")
+        frozen_part = lax.dot_general(
+            jnp.moveaxis(every_column, 0, 1).reshape(part_rows, tp_count * column_portion),
+            frozen_weight,
+            (((1,), (1,)), ((), ())),
+            preferred_element_type=jnp.float32,
+        )
+        gradient_rows = (frozen_part + adapter_output_rows).astype(jnp.bfloat16)
+        increment_high = adapter_increment.astype(jnp.bfloat16)
+        increment_low = (adapter_increment - increment_high.astype(jnp.float32)).astype(
+            jnp.bfloat16
+        )
         back = jnp.concatenate(
             [
-                adapter_output_rows.reshape(tok_count, BLOCK_TOKENS, width_portion),
-                adapter_increment.reshape(tok_count, BLOCK_TOKENS, column_portion),
+                gradient_rows.reshape(tok_count, BLOCK_TOKENS, width_portion),
+                increment_high.reshape(tok_count, BLOCK_TOKENS, column_portion),
+                increment_low.reshape(tok_count, BLOCK_TOKENS, column_portion),
             ],
             axis=2,
         )
@@ -146,7 +178,9 @@
         grad_down = down_add if grad_down is None else grad_down + down_add
         grad_up = up_add if grad_up is None else grad_up + up_add
     grad_up = stored_scale[:, None, None] * grad_up
-    returned = jnp.stack(returned_parts, axis=1).reshape(slots, BLOCK_TOKENS, lane)
+    returned = jnp.stack(returned_parts, axis=1).reshape(
+        slots, BLOCK_TOKENS, width_portion + 2 * column_portion
+    )
     mine = jnp.take(returned, destination, axis=0)
 
     base_out = lax.psum_scatter(
@@ -157,18 +191,11 @@
         scatter_dimension=0,
         tiled=True,
     ).T
-    frozen_input_gradient = lax.dot_general(
-        lax.all_gather(output_gradient, "tp", axis=1, tiled=True),
-        frozen_weight,
-        (((1,), (1,)), ((), ())),
-        preferred_element_type=jnp.float32,
-    )
-    projected = (
-        base_out + mine[:, :, width_portion:].reshape(token_rows, column_portion)
-    ).astype(jnp.bfloat16)
-    token_gradient = (
-        frozen_input_gradient + mine[:, :, :width_portion].reshape(token_rows, width_portion)
-    ).astype(jnp.bfloat16)
+    increment = mine[:, :, width_portion : width_portion + column_portion].astype(
+        jnp.float32
+    ) + mine[:, :, width_portion + column_portion :].astype(jnp.float32)
+    projected = (base_out + increment.reshape(token_rows, column_portion)).astype(jnp.bfloat16)
+    token_gradient = mine[:, :, :width_portion].reshape(token_rows, width_portion)
     return (projected, token_gradient, grad_down, grad_up)
 
 

time: 289 us -> 314 us (1.087)
  matrix products: 20.2 us -> 35.3 us
  starting transfers between devices: 26.2 us -> 40.7 us
  local copies, waits for them, and re-layouts: 27.5 us -> 22.3 us
    all_to_all x2, waiting for transfers between devices: 85.5 us -> 31.1 us  [owner_part(): lax.all_to_all(back, 'tok', split_axis=0, concat_axis=0, tiled=True)]
    ppermute x0 -> x6, waiting for transfers between devices: none -> 35.6 us  [tree_gather(): other = lax.ppermute(value, axis, pairs)]
    ppermute x6, waiting for transfers between devices: 14.8 us -> 32.8 us  [tree_sum(): value = value + lax.ppermute(value, axis, pairs)]
    ppermute x0 -> x6, starting transfers between devices: none -> 8.94 us  [tree_gather(): other = lax.ppermute(value, axis, pairs)]
    dot_general x1 -> x2, matrix products: 6.25 us -> 11.8 us  [owner_part(): lax.dot_general(jnp.moveaxis(every_column, 0, 1).reshape(part_rows, tp_co...]
    all_to_all x2, starting transfers between devices: 12 us -> 17.2 us  [owner_part(): lax.all_to_all(back, 'tok', split_axis=0, concat_axis=0, tiled=True)]
    transpose x0 -> x2, local copies, waits for them, and re-layouts: none -> 4.84 us  [owner_part(): jnp.moveaxis(every_column, 0, 1)]
  transfers between devices with their start and end apart: 11 -> 16, of which waited for: 6 -> 7; matrix products, arithmetic and copies ran while one was open for 20% -> 24% of each run, Pallas kernels for 0% -> 0%
where the time goes in v4:
time: 314 us; the launch traced here: 308 us
  waiting for transfers between devices  118 us (38%)
  blocking collectives  46.6 us (15%)
  starting transfers between devices  40.7 us (13%)
  matrix products  35.3 us (11%)
  other arithmetic  31.4 us (10%)
  local copies, waits for them, and re-layouts  22.3 us (7%)
  between operations  14.7 us (5%)
    all_to_all x1, blocking collectives, per_device(): lax.all_to_all(send[:, position], 'tok', split_axis=0, concat_axis=0, til...  46.6 us
    ppermute x6, waiting for transfers between devices, tree_gather(): other = lax.ppermute(value, axis, pairs)  35.6 us
    ppermute x6, waiting for transfers between devices, tree_sum(): value = value + lax.ppermute(value, axis, pairs)  32.8 us
    all_to_all x2, waiting for transfers between devices, owner_part(): lax.all_to_all(back, 'tok', split_axis=0, concat_axis=0, tiled=True)  31.1 us
    all_to_all x1, waiting for transfers between devices, per_device(): lax.all_to_all(send[:, position], 'tok', split_axis=0, concat_axis=0, til...  18 us
    all_to_all x2, starting transfers between devices, owner_part(): lax.all_to_all(back, 'tok', split_axis=0, concat_axis=0, tiled=True)  17.2 us
    dot_general x2, matrix products, owner_part(): lax.dot_general(jnp.moveaxis(every_column, 0, 1).reshape(part_rows, tp_co...  11.8 us
    ppermute x6, starting transfers between devices, tree_gather(): other = lax.ppermute(value, axis, pairs)  8.94 us
  transfers between devices with their start and end apart: 16, of which 7 were waited for; matrix products, arithmetic and copies ran while one was open for 24% of the time, Pallas kernels for 0%

profile of v4, /device:TPU:27, one launch (start us, length us, event | category | flops | bytes accessed | tf_op | source)
XLA Modules:
  0.0 308.5 jit_solution(16827139683132415007)
XLA Ops:
  12.8 2.4 gather_fusion.1
  15.2 2.3 select_select_fusion
  18.8 46.6 %all_to_all.20 = bf16[32,16,1408]{2,1,0:T(8,128)(2,1)} all-to-all(bf16[32,16,1408]{2,1,0:T(8,128)(2,1)S(1)} %get-tuple-element.46), channel_id=1, replica_groups=mesh['tok'=32,'tp'=8] {'tok'}, dimensions={0} | all-to-all | bytes 2883584 | tf_op jit(solution)/shard_map/all_to_all | solution.py:173
  65.4 5.9 %all-to-all-start.2 = ((bf16[32,16,1408]{2,1,0:T(8,128)(2,1)}), bf16[32,16,1408]{2,1,0:T(8,128)(2,1)S(1)}, u32[]{:S(2)}, u32[]{:S(2)}) async-start(bf16[32,16,1408]{2,1,0:T(8,128)(2,1)} %get-tuple-element.47), calls=%async_computation.3 | async-start | bytes 2883584 | tf_op jit(solution)/shard_map/all_to_all | solution.py:173
  71.4 6.5 %fusion.61 = f32[2048,512]{1,0:T(8,128)} fusion(bf16[1024,2048]{1,0:T(8,128)(2,1)} %param.11, bf16[512,1024]{1,0:T(8,128)(2,1)S(1)} %copy-done.6), kind=kOutput, calls=%fused_computation.131 | convolution fusion | flops 2147483648 | bytes 9437184 | tf_op jit(solution)/shard_map/dot_general | solution.py:187
  88.2 18.0 %all-to-all-done.2 = bf16[32,16,1408]{2,1,0:T(8,128)(2,1)S(1)} async-done(((bf16[32,16,1408]{2,1,0:T(8,128)(2,1)}), bf16[32,16,1408]{2,1,0:T(8,128)(2,1)S(1)}, u32[]{:S(2)}, u32[]{:S(2)}) %all-to-all-start.2) | async-done | bytes 1441824 | tf_op jit(solution)/shard_map/all_to_all | solution.py:173
  109.0 2.9 collective-permute-start
  120.5 14.6 %collective-permute-done.4 = f32[512,128]{0,1:T(8,128)S(1)} collective-permute-done((f32[512,128]{0,1:T(8,128)S(1)}, f32[512,128]{0,1:T(8,128)S(1)}, u32[]{:S(2)}, u32[]{:S(2)}) %collective-permute-start.4) | collective-permute-done | bytes 262176 | tf_op jit(solution)/shard_map/ppermute | solution.py:25
  141.0 2.1 collective-permute-start.2
  148.9 18.4 %collective-permute-done.2 = bf16[4,512,256]{2,1,0:T(8,128)(2,1)S(1)} collective-permute-done((bf16[4,512,256]{2,1,0:T(8,128)(2,1)S(1)}, bf16[4,512,256]{2,1,0:T(8,128)(2,1)S(1)}, u32[]{:S(2)}, u32[]{:S(2)}) %collective-permute-start.2) | collective-permute-done | bytes 1048608 | tf_op jit(solution)/shard_map/ppermute | solution.py:37
  167.6 2.4 copy.41
  170.0 5.9 %fusion.4 = bf16[512,1024]{1,0:T(8,128)(2,1)S(1)} fusion(f32[512,1024,1]{1,0,2:T(8,128)} %fusion.21, bf16[512,2048]{0,1:T(8,128)(2,1)} %bitcast.118, bf16[1024,2048]{1,0:T(8,128)(2,1)} %param.11), kind=kOutput, calls=%fused_computation.14 | convolution fusion | flops 2148532224 | bytes 9437184 | tf_op jit(solution)/shard_map/dot_general | solution.py:146
  177.3 7.6 %all-to-all-start.1 = ((bf16[32,16,1536]{2,1,0:T(8,128)(2,1)}), bf16[32,16,1536]{2,1,0:T(8,128)(2,1)}, u32[]{:S(2)}, u32[]{:S(2)}) async-start(bf16[32,16,1536]{2,1,0:T(8,128)(2,1)} %pad_maximum_fusion.1), calls=%async_computation.2 | async-start | bytes 3145728 | tf_op jit(solution)/shard_map/all_to_all | solution.py:165
  188.8 15.0 %collective-permute-done.10 = f32[512,128]{0,1:T(8,128)S(1)} collective-permute-done((f32[512,128]{0,1:T(8,128)S(1)}, f32[512,128]{0,1:T(8,128)S(1)}, u32[]{:S(2)}, u32[]{:S(2)}) %collective-permute-start.10) | collective-permute-done | bytes 262176 | tf_op jit(solution)/shard_map/ppermute | solution.py:25
  208.0 3.1 %collective-permute-done.11 = f32[512,128]{0,1:T(8,128)} collective-permute-done((f32[512,128]{0,1:T(8,128)S(1)}, f32[512,128]{0,1:T(8,128)}, u32[]{:S(2)}, u32[]{:S(2)}) %collective-permute-start.11) | collective-permute-done | bytes 262176 | tf_op jit(solution)/shard_map/ppermute | solution.py:25
  212.2 2.1 subtract_convert_fusion
  216.3 17.2 %collective-permute-done.8 = bf16[4,512,256]{2,1,0:T(8,128)(2,1)} collective-permute-done((bf16[4,512,256]{2,1,0:T(8,128)(2,1)S(1)}, bf16[4,512,256]{2,1,0:T(8,128)(2,1)}, u32[]{:S(2)}, u32[]{:S(2)}) %collective-permute-start.8) | collective-permute-done | bytes 1048608 | tf_op jit(solution)/shard_map/ppermute | solution.py:37
  233.6 2.6 fusion.2
  236.1 2.4 copy.44
  238.6 5.9 %fusion.3 = bf16[512,1024]{1,0:T(8,128)(2,1)S(1)} fusion(f32[512,1024,1]{1,0,2:T(8,128)} %fusion.14, bf16[512,2048]{0,1:T(8,128)(2,1)} %bitcast.119, bf16[1024,2048]{1,0:T(8,128)(2,1)} %param.11), kind=kOutput, calls=%fused_computation.12 | convolution fusion | flops 2148532224 | bytes 9437184 | tf_op jit(solution)/shard_map/dot_general | solution.py:146
  245.9 9.6 %all-to-all-start.3 = ((bf16[32,16,1536]{2,1,0:T(8,128)(2,1)}), bf16[32,16,1536]{2,1,0:T(8,128)(2,1)S(1)}, u32[]{:S(2)}, u32[]{:S(2)}) async-start(bf16[32,16,1536]{2,1,0:T(8,128)(2,1)} %pad_maximum_fusion.2), calls=%async_computation.4 | async-start | bytes 3145728 | tf_op jit(solution)/shard_map/all_to_all | solution.py:165
  261.0 31.1 %all-to-all-done.3 = bf16[32,16,1536]{2,1,0:T(8,128)(2,1)S(1)} async-done(((bf16[32,16,1536]{2,1,0:T(8,128)(2,1)}), bf16[32,16,1536]{2,1,0:T(8,128)(2,1)S(1)}, u32[]{:S(2)}, u32[]{:S(2)}) %all-to-all-start.3) | async-done | bytes 1572896 | tf_op jit(solution)/shard_map/all_to_all | solution.py:165
  292.1 3.4 %pad_maximum_fusion = bf16[32,2,16,1536]{3,2,1,0:T(8,128)(2,1)} fusion(bf16[32,1,16,1536]{3,2,1,0:T(8,128)(2,1)S(1)} %bitcast.109, bf16[32,1,16,1536]{3,2,1,0:T(8,128)(2,1)} %bitcast.22), kind=kLoop, calls=%fused_computation.3 | loop fusion | flops 1572864 | bytes 6291456 | tf_op jit(solution)/shard_map/stack | solution.py:181
  295.5 2.5 gather_fusion.2
  (167 shorter events, 63.2 us)
Async XLA Ops:
  7.2 77.0 %copy-start = (bf16[8,1024,64]{1,2,0:T(8,128)(2,1)S(1)}, bf16[8,1024,64]{1,2,0:T(8,128)(2,1)}, u32[]{:S(2)}) copy-start(bf16[8,1024,64]{1,2,0:T(8,128)(2,1)} %param.12) | copy-start | bytes 3145732
  65.4 40.8 %all-to-all-start.2 = ((bf16[32,16,1408]{2,1,0:T(8,128)(2,1)}), bf16[32,16,1408]{2,1,0:T(8,128)(2,1)S(1)}, u32[]{:S(2)}, u32[]{:S(2)}) async-start(bf16[32,16,1408]{2,1,0:T(8,128)(2,1)} %get-tuple-element.47), calls=%async_computation.3 | async-start | bytes 2883584 | tf_op jit(solution)/shard_map/all_to_all | solution.py:173
  71.3 228.4 %reduce-scatter.2.cloned.1.call-start = ((), (), s32[]{:S(2)}) async-start(), calls=%async_computation.5 | async-start | bytes 4718592 | tf_op jit(solution)/shard_map/reduce_scatter | solution.py:186
  81.4 37.1 %copy-start.19 = (pred[32,8]{0,1:T(8,128)(4,1)}, pred[32,8]{0,1:T(8,128)(4,1)S(1)}, u32[]{:S(2)}) copy-start(pred[32,8]{0,1:T(8,128)(4,1)S(1)} %get-tuple-element.50) | copy-start | bytes 772
  84.1 30.6 %copy-start.7 = (bf16[32,16,256]{2,1,0:T(8,128)(2,1)}, bf16[32,16,256]{2,1,0:T(8,128)(2,1)S(1)}, u32[]{:S(2)}) copy-start(bf16[32,16,256]{2,1,0:T(8,128)(2,1)S(1)} %slice.86) | copy-start | bytes 786436
  86.3 30.2 %collective-permute-start.3 = (f32[512,128]{0,1:T(8,128)}, f32[512,128]{0,1:T(8,128)}, u32[]{:S(2)}, u32[]{:S(2)}) collective-permute-start(f32[512,128]{0,1:T(8,128)} %pad_maximum_fusion.3), channel_id=1, source_target_pairs={{0,1},{1,0},{2,3},{3,2},{4,5},{5,4},{6,7},{7,6},{8,9},{9,8},{10,11... | collective-permute-start | bytes 786440 | tf_op jit(solution)/shard_map/ppermute | solution.py:25
  109.0 5.7 %collective-permute-start = (bf16[1,512,256]{2,1,0:T(8,128)(2,1)S(1)}, bf16[1,512,256]{2,1,0:T(8,128)(2,1)}, u32[]{:S(2)}, u32[]{:S(2)}) collective-permute-start(bf16[1,512,256]{2,1,0:T(8,128)(2,1)S(1)} %bitcast.128), channel_id=1, source_target_pairs={{0,1},{1,0},{2,3},{3,2},{4,5},{5,4},{6,7},{7,6},{8,9},{9,8},{10,11... | collective-permute-start | bytes 786440 | tf_op jit(solution)/shard_map/ppermute | solution.py:37
  114.8 21.4 %copy-start.22 = (f32[8]{0:T(128)S(1)}, f32[8]{0:T(128)}, u32[]{:S(2)}) copy-start(f32[8]{0:T(128)} %compare_select_fusion.4) | copy-start | bytes 100
  115.9 24.9 %collective-permute-start.1 = (bf16[2,512,256]{2,1,0:T(8,128)(2,1)S(1)}, bf16[2,512,256]{2,1,0:T(8,128)(2,1)S(1)}, u32[]{:S(2)}, u32[]{:S(2)}) collective-permute-start(bf16[2,512,256]{2,1,0:T(8,128)(2,1)S(1)} %maximum_select_fusion.4), channel_id=1, source_target_pairs={{0,2},{1,3},{2,0},{3,1},{4,6},{5,7},{6,4},{7,5},{8,10},{9,11},{10,... | collective-permute-start | bytes 1572872 | tf_op jit(solution)/shard_map/ppermute | solution.py:37
  117.5 17.7 %collective-permute-start.4 = (f32[512,128]{0,1:T(8,128)S(1)}, f32[512,128]{0,1:T(8,128)S(1)}, u32[]{:S(2)}, u32[]{:S(2)}) collective-permute-start(f32[512,128]{0,1:T(8,128)S(1)} %fusion.60), channel_id=1, source_target_pairs={{0,2},{1,3},{2,0},{3,1},{4,6},{5,7},{6,4},{7,5},{8,10},{9,11},{10,... | collective-permute-start | bytes 786440 | tf_op jit(solution)/shard_map/ppermute | solution.py:25
  135.2 8.7 %collective-permute-start.5 = (f32[512,128]{0,1:T(8,128)S(1)}, f32[512,128]{0,1:T(8,128)S(1)}, u32[]{:S(2)}, u32[]{:S(2)}) collective-permute-start(f32[512,128]{0,1:T(8,128)S(1)} %add.150), channel_id=1, source_target_pairs={{0,4},{1,5},{2,6},{3,7},{4,0},{5,1},{6,2},{7,3},{8,12},{9,13},{10,... | collective-permute-start | bytes 786440 | tf_op jit(solution)/shard_map/ppermute | solution.py:25
  139.5 45.4 %collective-permute-start.6 = (bf16[1,512,256]{2,1,0:T(8,128)(2,1)S(1)}, bf16[1,512,256]{2,1,0:T(8,128)(2,1)}, u32[]{:S(2)}, u32[]{:S(2)}) collective-permute-start(bf16[1,512,256]{2,1,0:T(8,128)(2,1)S(1)} %bitcast.115), channel_id=1, source_target_pairs={{0,1},{1,0},{2,3},{3,2},{4,5},{5,4},{6,7},{7,6},{8,9},{9,8},{10,11... | collective-permute-start | bytes 786440 | tf_op jit(solution)/shard_map/ppermute | solution.py:37
  141.0 26.3 %collective-permute-start.2 = (bf16[4,512,256]{2,1,0:T(8,128)(2,1)S(1)}, bf16[4,512,256]{2,1,0:T(8,128)(2,1)S(1)}, u32[]{:S(2)}, u32[]{:S(2)}) collective-permute-start(bf16[4,512,256]{2,1,0:T(8,128)(2,1)S(1)} %maximum_select_fusion.2), channel_id=1, source_target_pairs={{0,4},{1,5},{2,6},{3,7},{4,0},{5,1},{6,2},{7,3},{8,12},{9,13},{10,... | collective-permute-start | bytes 3145736 | tf_op jit(solution)/shard_map/ppermute | solution.py:37
  143.9 42.3 %collective-permute-start.9 = (f32[512,128]{0,1:T(8,128)}, f32[512,128]{0,1:T(8,128)}, u32[]{:S(2)}, u32[]{:S(2)}) collective-permute-start(f32[512,128]{0,1:T(8,128)} %pad_maximum_fusion.4), channel_id=1, source_target_pairs={{0,1},{1,0},{2,3},{3,2},{4,5},{5,4},{6,7},{7,6},{8,9},{9,8},{10,11... | collective-permute-start | bytes 786440 | tf_op jit(solution)/shard_map/ppermute | solution.py:25
  177.3 68.6 %all-to-all-start.1 = ((bf16[32,16,1536]{2,1,0:T(8,128)(2,1)}), bf16[32,16,1536]{2,1,0:T(8,128)(2,1)}, u32[]{:S(2)}, u32[]{:S(2)}) async-start(bf16[32,16,1536]{2,1,0:T(8,128)(2,1)} %pad_maximum_fusion.1), calls=%async_computation.2 | async-start | bytes 3145728 | tf_op jit(solution)/shard_map/all_to_all | solution.py:165
  186.0 21.4 %copy-start.17 = (s32[32,16]{0,1:T(8,128)S(1)}, s32[32,16]{0,1:T(8,128)}, u32[]{:S(2)}) copy-start(s32[32,16]{0,1:T(8,128)} %get-tuple-element.37) | copy-start | bytes 6148
  186.0 21.5 %copy-start.21 = (bf16[32,8]{0,1:T(8,128)(2,1)S(1)}, bf16[32,8]{0,1:T(8,128)(2,1)}, u32[]{:S(2)}) copy-start(bf16[32,8]{0,1:T(8,128)(2,1)} %get-tuple-element.51) | copy-start | bytes 1540
  186.1 21.8 %copy-start.18 = (f32[32,16]{0,1:T(8,128)S(1)}, f32[32,16]{0,1:T(8,128)}, u32[]{:S(2)}) copy-start(f32[32,16]{0,1:T(8,128)} %get-tuple-element.35) | copy-start | bytes 6148
  186.1 19.2 %collective-permute-start.7 = (bf16[2,512,256]{2,1,0:T(8,128)(2,1)S(1)}, bf16[2,512,256]{2,1,0:T(8,128)(2,1)S(1)}, u32[]{:S(2)}, u32[]{:S(2)}) collective-permute-start(bf16[2,512,256]{2,1,0:T(8,128)(2,1)S(1)} %maximum_select_fusion.5), channel_id=1, source_target_pairs={{0,2},{1,3},{2,0},{3,1},{4,6},{5,7},{6,4},{7,5},{8,10},{9,11},{10,... | collective-permute-start | bytes 1572872 | tf_op jit(solution)/shard_map/ppermute | solution.py:37
  187.2 16.6 %collective-permute-start.10 = (f32[512,128]{0,1:T(8,128)S(1)}, f32[512,128]{0,1:T(8,128)S(1)}, u32[]{:S(2)}, u32[]{:S(2)}) collective-permute-start(f32[512,128]{0,1:T(8,128)S(1)} %add.153), channel_id=1, source_target_pairs={{0,2},{1,3},{2,0},{3,1},{4,6},{5,7},{6,4},{7,5},{8,10},{9,11},{10,... | collective-permute-start | bytes 786440 | tf_op jit(solution)/shard_map/ppermute | solution.py:25
  203.8 7.3 %collective-permute-start.11 = (f32[512,128]{0,1:T(8,128)S(1)}, f32[512,128]{0,1:T(8,128)}, u32[]{:S(2)}, u32[]{:S(2)}) collective-permute-start(f32[512,128]{0,1:T(8,128)S(1)} %add.154), channel_id=1, source_target_pairs={{0,4},{1,5},{2,6},{3,7},{4,0},{5,1},{6,2},{7,3},{8,12},{9,13},{10,... | collective-permute-start | bytes 786440 | tf_op jit(solution)/shard_map/ppermute | solution.py:25
  205.4 11.0 %copy-start.2 = (bf16[4,512,256]{2,1,0:T(8,128)(2,1)}, bf16[4,512,256]{2,1,0:T(8,128)(2,1)S(1)}, u32[]{:S(2)}) copy-start(bf16[4,512,256]{2,1,0:T(8,128)(2,1)S(1)} %maximum_select_fusion.3) | copy-start | bytes 3145732
  205.4 28.2 %collective-permute-start.8 = (bf16[4,512,256]{2,1,0:T(8,128)(2,1)S(1)}, bf16[4,512,256]{2,1,0:T(8,128)(2,1)}, u32[]{:S(2)}, u32[]{:S(2)}) collective-permute-start(bf16[4,512,256]{2,1,0:T(8,128)(2,1)S(1)} %maximum_select_fusion.3), channel_id=1, source_target_pairs={{0,4},{1,5},{2,6},{3,7},{4,0},{5,1},{6,2},{7,3},{8,12},{9,13},{10,... | collective-permute-start | bytes 3145736 | tf_op jit(solution)/shard_map/ppermute | solution.py:37
  245.9 46.2 %all-to-all-start.3 = ((bf16[32,16,1536]{2,1,0:T(8,128)(2,1)}), bf16[32,16,1536]{2,1,0:T(8,128)(2,1)S(1)}, u32[]{:S(2)}, u32[]{:S(2)}) async-start(bf16[32,16,1536]{2,1,0:T(8,128)(2,1)} %pad_maximum_fusion.2), calls=%async_computation.4 | async-start | bytes 3145728 | tf_op jit(solution)/shard_map/all_to_all | solution.py:165
  (22 other events, 99.8 us)
Sparse Core Ops, SparseCore 0:
  78.1 41.3 reduce-scatter.1

commit v5 on v0

--- a/solution.py
+++ b/solution.py
@@ -58,7 +58,12 @@
         preferred_element_type=jnp.float32,
     ).astype(jnp.bfloat16)
     slot_adapter = jnp.sum(jnp.where(placement, local_index[None, :] + 1, 0), axis=1) - 1
-    arrived_rows, arrived_grads, arrived_adapter = (
+    tag = jnp.zeros((storage_position_count, BLOCK_TOKENS, 128), jnp.bfloat16)
+    tag = tag.at[:, 0, 0].set((slot_adapter + 1).astype(jnp.bfloat16))
+    tagged_grads = jnp.concatenate(
+        [send_grads.reshape(storage_position_count, BLOCK_TOKENS, column_portion), tag], axis=2
+    )
+    arrived_rows, arrived_tagged = (
         lax.all_to_all(
             send_rows.reshape(storage_position_count, BLOCK_TOKENS, width_portion),
             "tok",
@@ -66,15 +71,10 @@
             concat_axis=0,
             tiled=True,
         ),
-        lax.all_to_all(
-            send_grads.reshape(storage_position_count, BLOCK_TOKENS, column_portion),
-            "tok",
-            split_axis=0,
-            concat_axis=0,
-            tiled=True,
-        ),
-        lax.all_to_all(slot_adapter, "tok", split_axis=0, concat_axis=0, tiled=True),
+        lax.all_to_all(tagged_grads, "tok", split_axis=0, concat_axis=0, tiled=True),
     )
+    arrived_grads = arrived_tagged[:, :, :column_portion]
+    arrived_adapter = arrived_tagged[:, 0, column_portion].astype(jnp.int32) - 1
     row_total = storage_position_count * BLOCK_TOKENS
     input_row_block = arrived_rows.reshape(row_total, width_portion)
     gradient_row_block = arrived_grads.reshape(row_total, column_portion)
@@ -122,22 +122,21 @@
     adapter_output_rows = jnp.einsum(
         "ymf,mcf->yc", gradient_picked, adapter_down_matrices, preferred_element_type=jnp.float32
     )
-    delta_back, row_input_gradient = (
-        lax.all_to_all(
-            adapter_increment.reshape(storage_position_count, BLOCK_TOKENS, column_portion),
-            "tok",
-            split_axis=0,
-            concat_axis=0,
-            tiled=True,
+    returned = lax.all_to_all(
+        jnp.concatenate(
+            [
+                adapter_output_rows.reshape(storage_position_count, BLOCK_TOKENS, width_portion),
+                adapter_increment.reshape(storage_position_count, BLOCK_TOKENS, column_portion),
+            ],
+            axis=2,
         ),
-        lax.all_to_all(
-            adapter_output_rows.reshape(storage_position_count, BLOCK_TOKENS, width_portion),
-            "tok",
-            split_axis=0,
-            concat_axis=0,
-            tiled=True,
-        ),
+        "tok",
+        split_axis=0,
+        concat_axis=0,
+        tiled=True,
     )
+    row_input_gradient = returned[:, :, :width_portion]
+    delta_back = returned[:, :, width_portion:]
     adapter_input_gradient = jnp.take(row_input_gradient, destination, axis=0)
     mine_delta = jnp.take(delta_back, destination, axis=0)
     projected = (base_out + mine_delta.reshape(token_rows, column_portion)).astype(jnp.bfloat16)

time: 283 us -> 320 us (1.13)
  waiting for transfers between devices: 159 us -> 192 us
  starting transfers between devices: 34.5 us -> 26.3 us
  other arithmetic: 4.8 us -> 11.3 us
  local copies, waits for them, and re-layouts: 12.7 us -> 17.8 us
    psum x1, waiting for transfers between devices: 0.02 us -> 59.4 us  [per_device(): low_sum, pull_sum = lax.psum((low_part, pull_part), 'tp')]
    all_to_all x1, waiting for transfers between devices: 35 us -> 0.01 us  [per_device(): lax.all_to_all(send_rows.reshape(storage_position_count, BLOCK_TOKENS, wi...]
    all_to_all x4 -> x2, waiting for transfers between devices: 124 us -> 132 us  [the longest x1 116 us: per_device(): lax.all_to_all(jnp.concatenate([adapter_output_rows.reshape(storage_posit...]
    all_to_all x4 -> x2, starting transfers between devices: 27.8 us -> 20.7 us  [the longest x1 11 us: per_device(): lax.all_to_all(tagged_grads, 'tok', split_axis=0, concat_axis=0, tiled=True)]
    slice x0 -> x3, local copies, waits for them, and re-layouts: none -> 6.11 us  [the longest x1 4.79 us: per_device(): row_input_gradient = returned[:, :, :width_portion]]
    concatenate x0 -> x2, other arithmetic: none -> 6.06 us  [the longest x1 5.09 us: per_device(): jnp.concatenate([adapter_output_rows.reshape(storage_position_count, BLOC...]
  transfers between devices with their start and end apart: 8 -> 6, of which waited for: 5 -> 3; matrix products, arithmetic and copies ran while one was open for 13% -> 15% of each run, Pallas kernels for 0% -> 0%
where the time goes in v5:
time: 320 us; the launch traced here: 317 us
  waiting for transfers between devices  192 us (60%)
  matrix products  28.3 us (9%)
  blocking collectives  27.2 us (8%)
  starting transfers between devices  26.3 us (8%)
  local copies, waits for them, and re-layouts  17.8 us (6%)
  between operations  14 us (4%)
  other arithmetic  11.3 us (4%)
    all_to_all x1, waiting for transfers between devices, per_device(): lax.all_to_all(jnp.concatenate([adapter_output_rows.reshape(storage_posit...  116 us
    psum x1, waiting for transfers between devices, per_device(): low_sum, pull_sum = lax.psum((low_part, pull_part), 'tp')  59.4 us
    psum x1, blocking collectives, per_device(): low_sum, pull_sum = lax.psum((low_part, pull_part), 'tp')  27.2 us
    all_to_all x1, waiting for transfers between devices, per_device(): lax.all_to_all(tagged_grads, 'tok', split_axis=0, concat_axis=0, tiled=True)  16.5 us
    all_to_all x1, starting transfers between devices, per_device(): lax.all_to_all(tagged_grads, 'tok', split_axis=0, concat_axis=0, tiled=True)  11 us
    all_to_all x1, starting transfers between devices, per_device(): lax.all_to_all(jnp.concatenate([adapter_output_rows.reshape(storage_posit...  9.63 us
    dot_general x1, matrix products, per_device(): lax.dot_general(weight_cols, tokens, (((0,), (1,)), ((), ())), preferred_...  6.67 us
  transfers between devices with their start and end apart: 6, of which 3 were waited for; matrix products, arithmetic and copies ran while one was open for 15% of the time, Pallas kernels for 0%

profile of v5, /device:TPU:27, one launch (start us, length us, event | category | flops | bytes accessed | tf_op | source)
XLA Modules:
  0.0 317.2 jit_solution(16250406826348366488)
XLA Ops:
  8.6 1.1 reshape.268
  11.1 11.0 %all-to-all-start = ((bf16[64,16,384]{2,1,0:T(8,128)(2,1)}), bf16[64,16,384]{2,1,0:T(8,128)(2,1)S(1)}, u32[]{:S(2)}, u32[]{:S(2)}) async-start(bf16[64,16,384]{2,1,0:T(8,128)(2,1)} %fusion.19), calls=%async_computation.1 | async-start | bytes 1572864 | tf_op jit(solution)/shard_map/all_to_all | solution.py:74
  22.2 1.6 reshape.272
  24.6 2.5 copy.36
  27.1 16.5 %all-to-all-done = bf16[64,16,384]{2,1,0:T(8,128)(2,1)S(1)} async-done(((bf16[64,16,384]{2,1,0:T(8,128)(2,1)}), bf16[64,16,384]{2,1,0:T(8,128)(2,1)S(1)}, u32[]{:S(2)}, u32[]{:S(2)}) %all-to-all-start) | async-done | bytes 786464 | tf_op jit(solution)/shard_map/all_to_all | solution.py:74
  43.6 5.5 %all-to-all-start.1 = ((bf16[64,16,1024]{2,1,0:T(8,128)(2,1)}), bf16[64,16,1024]{2,1,0:T(8,128)(2,1)}, u32[]{:S(2)}, u32[]{:S(2)}) async-start(bf16[64,16,1024]{2,1,0:T(8,128)(2,1)} %bitcast.28), calls=%async_computation.2 | async-start | bytes 4194304 | tf_op jit(solution)/shard_map/all_to_all | solution.py:67
  49.2 1.2 fusion.30
  50.8 2.2 multiply_reduce_fusion.1
  53.1 6.7 %fusion.38 = f32[2048,512]{1,0:T(8,128)} fusion(bf16[1024,2048]{1,0:T(8,128)(2,1)} %param.11, bf16[512,1024]{1,0:T(8,128)(2,1)S(1)} %copy-done.1), kind=kOutput, calls=%fused_computation.76 | convolution fusion | flops 2147483648 | bytes 9437184 | tf_op jit(solution)/shard_map/dot_general | solution.py:32
  61.5 59.4 %all-reduce.4.cloned.1.call-done = f32[1024,64]{0,1:T(8,128)} async-done(((f32[1024,64]{0,1:T(8,128)}), f32[1024,64]{0,1:T(8,128)}) %all-reduce.4.cloned.1.call-update) | async-done | bytes 262160 | tf_op jit(solution)/shard_map/psum | solution.py:106
  120.8 1.0 multiply_convert_fusion
  121.8 3.2 %fusion.8 = f32[1024,1024,1]{1,0,2:T(8,128)} fusion(bf16[8,1024,64]{1,2,0:T(8,128)(2,1)S(1)} %copy-done, bf16[1024,64]{0,1:T(8,128)(2,1)S(1)} %multiply_convert_fusion, bf16[1024,8]{0,1:T(8,128)(2,1)S(1)} %convert_element_type.80), kind=kOutput, calls=%fused_computation.18 | convolution fusion | flops 1074266112 | bytes 5390336 | tf_op jit(solution)/shard_map/ymf,mcf->yc/dot_general | solution.py:122
  125.1 2.9 fusion.39
  128.2 27.2 %all-reduce.5 = bf16[1024,64]{0,1:T(8,128)(2,1)S(1)} all-reduce(f32[1024,64]{0,1:T(8,128)S(1)} %multiply_reduce_fusion), channel_id=1, replica_groups=mesh['tok'=32,'tp'=8] {'tp'}, use_global_device_ids=true, to_apply=%region_10.11 | all-reduce | flops 65536 | bytes 393216 | tf_op jit(solution)/shard_map/psum | solution.py:106
  156.0 5.1 %pad_maximum_fusion = f32[64,16,1280]{2,1,0:T(8,128)} fusion(f32[64,16,256]{2,1,0:T(8,128)S(1)} %bitcast.78, f32[64,16,1024]{2,1,0:T(8,128)} %bitcast.73), kind=kLoop, calls=%fused_computation.3 | loop fusion | flops 1310720 | bytes 10485760 | tf_op jit(solution)/shard_map/concatenate | solution.py:126
  161.1 9.6 %all-to-all-start.2 = ((f32[64,16,1280]{2,1,0:T(8,128)}), f32[64,16,1280]{2,1,0:T(8,128)}, u32[]{:S(2)}, u32[]{:S(2)}) async-start(f32[64,16,1280]{2,1,0:T(8,128)} %pad_maximum_fusion), calls=%async_computation.3 | async-start | bytes 10485760 | tf_op jit(solution)/shard_map/all_to_all | solution.py:125
  171.6 1.2 fusion.16
  172.9 4.2 %convolution_bitcast_fusion = f32[8,1024,64]{1,2,0:T(8,128)} fusion(bf16[1024,1024,1]{1,0,2:T(8,128)(2,1)} %bitcast.17, bf16[1024,64]{0,1:T(8,128)(2,1)S(1)} %multiply_convert_fusion, bf16[1024,8]{0,1:T(8,128)(2,1)S(1)} %convert_element_type.80), kind=kOutput, calls=%fused_computation.10 | convolution fusion | flops 1074266112 | bytes 4341760 | tf_op jit(solution)/shard_map/rd,rak->adk/dot_general | solution.py:116
  177.0 115.6 %all-to-all-done.2 = f32[64,16,1280]{2,1,0:T(8,128)} async-done(((f32[64,16,1280]{2,1,0:T(8,128)}), f32[64,16,1280]{2,1,0:T(8,128)}, u32[]{:S(2)}, u32[]{:S(2)}) %all-to-all-start.2) | async-done | bytes 5242912 | tf_op jit(solution)/shard_map/all_to_all | solution.py:125
  292.7 1.3 slice.41
  294.8 1.1 fusion.20
  296.8 4.8 %slice.42 = f32[64,16,1024]{2,1,0:T(8,128)} slice(f32[64,16,1280]{2,1,0:T(8,128)} %all-to-all-done.2), slice={[0:64], [0:16], [0:1024]} | slice | bytes 8388608 | tf_op jit(solution)/shard_map/slice | solution.py:138
  301.6 2.9 gather_fusion.1
  304.5 6.2 %fusion.1 = bf16[512,1024]{1,0:T(8,128)(2,1)} fusion(f32[32,16,1024]{2,1,0:T(8,128)S(1)} %gather_fusion.1, bf16[512,2048]{1,0:T(8,128)(2,1)} %all-gather.2.cloned.1.call-done, bf16[1024,2048]{1,0:T(8,128)(2,1)} %param.11, pred[512]{0:T(512)(128)(4,1)S(1)} %broadcast_in_dim.123), kind=kOutput, calls=%fused_computation.7 | convolution fusion | flops 2149056512 | bytes 9437696 | tf_op jit(solution)/shard_map/dot_general | solution.py:144
  (55 shorter events, 9.2 us)
Async XLA Ops:
  7.2 114.7 %copy-start = (bf16[8,1024,64]{1,2,0:T(8,128)(2,1)S(1)}, bf16[8,1024,64]{1,2,0:T(8,128)(2,1)}, u32[]{:S(2)}) copy-start(bf16[8,1024,64]{1,2,0:T(8,128)(2,1)} %param.12) | copy-start | bytes 3145732
  11.1 32.4 %all-to-all-start = ((bf16[64,16,384]{2,1,0:T(8,128)(2,1)}), bf16[64,16,384]{2,1,0:T(8,128)(2,1)S(1)}, u32[]{:S(2)}, u32[]{:S(2)}) async-start(bf16[64,16,384]{2,1,0:T(8,128)(2,1)} %fusion.19), calls=%async_computation.1 | async-start | bytes 1572864 | tf_op jit(solution)/shard_map/all_to_all | solution.py:74
  43.6 81.5 %all-to-all-start.1 = ((bf16[64,16,1024]{2,1,0:T(8,128)(2,1)}), bf16[64,16,1024]{2,1,0:T(8,128)(2,1)}, u32[]{:S(2)}, u32[]{:S(2)}) async-start(bf16[64,16,1024]{2,1,0:T(8,128)(2,1)} %bitcast.28), calls=%async_computation.2 | async-start | bytes 4194304 | tf_op jit(solution)/shard_map/all_to_all | solution.py:67
  49.1 71.7 %all-reduce.4.cloned.1.call-start = ((), (), s32[]{:S(2)}) async-start(), calls=%async_computation.5 | async-start | bytes 524288 | tf_op jit(solution)/shard_map/psum | solution.py:106
  50.7 2.4 copy-start.1
  53.0 241.8 %reduce-scatter.2.cloned.1.call-start = ((), (), s32[]{:S(2)}) async-start(), calls=%async_computation.4 | async-start | bytes 4718592 | tf_op jit(solution)/shard_map/reduce_scatter | solution.py:31
  59.7 0.7 copy-start.2
  59.7 0.7 copy-start.3
  127.9 27.5 %copy-start.4 = (bf16[8,64,256]{2,1,0:T(8,128)(2,1)S(1)}, bf16[8,64,256]{2,1,0:T(8,128)(2,1)}, u32[]{:S(2)}) copy-start(bf16[8,64,256]{2,1,0:T(8,128)(2,1)} %param.13) | copy-start | bytes 786436
  161.1 131.6 %all-to-all-start.2 = ((f32[64,16,1280]{2,1,0:T(8,128)}), f32[64,16,1280]{2,1,0:T(8,128)}, u32[]{:S(2)}, u32[]{:S(2)}) async-start(f32[64,16,1280]{2,1,0:T(8,128)} %pad_maximum_fusion), calls=%async_computation.3 | async-start | bytes 10485760 | tf_op jit(solution)/shard_map/all_to_all | solution.py:125
  170.7 133.8 %all-gather.2.cloned.1.call-start = ((), (), s32[]{:S(2)}) async-start(), calls=%async_computation.6 | async-start | bytes 2359296 | tf_op jit(solution)/shard_map/all_gather | solution.py:145
Sparse Core Ops, SparseCore 0:
  53.1 67.6 all-reduce.3
  123.4 40.8 reduce-scatter.1
  173.3 30.2 all-gather.1

commit v6 on v5

--- a/solution.py
+++ b/solution.py
@@ -63,15 +63,14 @@
     tagged_grads = jnp.concatenate(
         [send_grads.reshape(storage_position_count, BLOCK_TOKENS, column_portion), tag], axis=2
     )
-    arrived_rows, arrived_tagged = (
-        lax.all_to_all(
-            send_rows.reshape(storage_position_count, BLOCK_TOKENS, width_portion),
-            "tok",
-            split_axis=0,
-            concat_axis=0,
-            tiled=True,
-        ),
-        lax.all_to_all(tagged_grads, "tok", split_axis=0, concat_axis=0, tiled=True),
+    arrived_tagged = lax.all_to_all(tagged_grads, "tok", split_axis=0, concat_axis=0, tiled=True)
+    send_rows, arrived_tagged = lax.optimization_barrier((send_rows, arrived_tagged))
+    arrived_rows = lax.all_to_all(
+        send_rows.reshape(storage_position_count, BLOCK_TOKENS, width_portion),
+        "tok",
+        split_axis=0,
+        concat_axis=0,
+        tiled=True,
     )
     arrived_grads = arrived_tagged[:, :, :column_portion]
     arrived_adapter = arrived_tagged[:, 0, column_portion].astype(jnp.int32) - 1

time: 320 us -> 324 us (1.012)
  no operation moved by 1% of the time
where the time goes in v6:
time: 324 us; the launch traced here: 322 us
  waiting for transfers between devices  193 us (60%)
  matrix products  28.7 us (9%)
  blocking collectives  27.7 us (9%)
  starting transfers between devices  26.5 us (8%)
  local copies, waits for them, and re-layouts  19.9 us (6%)
  between operations  14.1 us (4%)
  other arithmetic  12.2 us (4%)
    all_to_all x1, waiting for transfers between devices, per_device(): lax.all_to_all(jnp.concatenate([adapter_output_rows.reshape(storage_posit...  116 us
    psum x1, waiting for transfers between devices, per_device(): low_sum, pull_sum = lax.psum((low_part, pull_part), 'tp')  58.8 us
    psum x1, blocking collectives, per_device(): low_sum, pull_sum = lax.psum((low_part, pull_part), 'tp')  27.7 us
    all_to_all x1, waiting for transfers between devices, per_device(): lax.all_to_all(tagged_grads, 'tok', split_axis=0, concat_axis=0, tiled=True)  18.1 us
    all_to_all x1, starting transfers between devices, per_device(): lax.all_to_all(tagged_grads, 'tok', split_axis=0, concat_axis=0, tiled=True)  11.1 us
    all_to_all x1, starting transfers between devices, per_device(): lax.all_to_all(jnp.concatenate([adapter_output_rows.reshape(storage_posit...  9.76 us
    dot_general x1, matrix products, per_device(): lax.dot_general(weight_cols, tokens, (((0,), (1,)), ((), ())), preferred_...  6.97 us
  transfers between devices with their start and end apart: 6, of which 3 were waited for; matrix products, arithmetic and copies ran while one was open for 15% of the time, Pallas kernels for 0%

profile of v6, /device:TPU:27, one launch (start us, length us, event | category | flops | bytes accessed | tf_op | source)
XLA Modules:
  0.0 322.3 jit_solution(13112738963379048208)
XLA Ops:
  11.7 11.1 %all-to-all-start = ((bf16[64,16,384]{2,1,0:T(8,128)(2,1)}), bf16[64,16,384]{2,1,0:T(8,128)(2,1)}, u32[]{:S(2)}, u32[]{:S(2)}) async-start(bf16[64,16,384]{2,1,0:T(8,128)(2,1)} %fusion.19), calls=%async_computation.1 | async-start | bytes 1572864 | tf_op jit(solution)/shard_map/all_to_all | solution.py:66
  22.8 1.3 reshape.268
  24.1 2.0 convolution_convert_fusion
  26.1 18.1 %all-to-all-done = bf16[64,16,384]{2,1,0:T(8,128)(2,1)} async-done(((bf16[64,16,384]{2,1,0:T(8,128)(2,1)}), bf16[64,16,384]{2,1,0:T(8,128)(2,1)}, u32[]{:S(2)}, u32[]{:S(2)}) %all-to-all-start) | async-done | bytes 786464 | tf_op jit(solution)/shard_map/all_to_all | solution.py:66
  44.2 2.5 copy.36
  46.7 5.5 %all-to-all-start.1 = ((bf16[64,16,1024]{2,1,0:T(8,128)(2,1)}), bf16[64,16,1024]{2,1,0:T(8,128)(2,1)S(1)}, u32[]{:S(2)}, u32[]{:S(2)}) async-start(bf16[64,16,1024]{2,1,0:T(8,128)(2,1)} %bitcast.28), calls=%async_computation.2 | async-start | bytes 4194304 | tf_op jit(solution)/shard_map/all_to_all | solution.py:68
  52.3 1.9 slice.32
  54.1 2.1 add_reduce_fusion
  56.6 2.3 multiply_reduce_fusion.1
  58.9 7.0 %fusion.36 = f32[2048,512]{1,0:T(8,128)} fusion(bf16[1024,2048]{1,0:T(8,128)(2,1)} %param.11, bf16[512,1024]{1,0:T(8,128)(2,1)} %param.10), kind=kOutput, calls=%fused_computation.74 | convolution fusion | flops 2147483648 | bytes 9437184 | tf_op jit(solution)/shard_map/dot_general | solution.py:32
  67.6 58.8 %all-reduce.4.cloned.1.call-done = f32[1024,64]{0,1:T(8,128)} async-done(((f32[1024,64]{0,1:T(8,128)}), f32[1024,64]{0,1:T(8,128)}) %all-reduce.4.cloned.1.call-update) | async-done | bytes 262160 | tf_op jit(solution)/shard_map/psum | solution.py:105
  127.4 3.2 fusion.8
  130.6 1.3 fusion.37
  132.2 27.7 %all-reduce.5 = bf16[1024,64]{0,1:T(8,128)(2,1)S(1)} all-reduce(f32[1024,64]{0,1:T(8,128)S(1)} %multiply_reduce_fusion), channel_id=1, replica_groups=mesh['tok'=32,'tp'=8] {'tp'}, use_global_device_ids=true, to_apply=%region_10.11 | all-reduce | flops 65536 | bytes 393216 | tf_op jit(solution)/shard_map/psum | solution.py:105
  159.9 1.5 fusion.13
  161.4 5.1 %pad_maximum_fusion = f32[64,16,1280]{2,1,0:T(8,128)} fusion(f32[64,16,256]{2,1,0:T(8,128)S(1)} %bitcast.80, f32[64,16,1024]{2,1,0:T(8,128)} %bitcast.73), kind=kLoop, calls=%fused_computation.3 | loop fusion | flops 1310720 | bytes 10485760 | tf_op jit(solution)/shard_map/concatenate | solution.py:125
  166.5 9.8 %all-to-all-start.2 = ((f32[64,16,1280]{2,1,0:T(8,128)}), f32[64,16,1280]{2,1,0:T(8,128)}, u32[]{:S(2)}, u32[]{:S(2)}) async-start(f32[64,16,1280]{2,1,0:T(8,128)} %pad_maximum_fusion), calls=%async_computation.3 | async-start | bytes 10485760 | tf_op jit(solution)/shard_map/all_to_all | solution.py:124
  177.2 2.3 fusion.16
  179.5 2.6 convolution_bitcast_fusion
  182.1 115.7 %all-to-all-done.2 = f32[64,16,1280]{2,1,0:T(8,128)} async-done(((f32[64,16,1280]{2,1,0:T(8,128)}), f32[64,16,1280]{2,1,0:T(8,128)}, u32[]{:S(2)}, u32[]{:S(2)}) %all-to-all-start.2) | async-done | bytes 5242912 | tf_op jit(solution)/shard_map/all_to_all | solution.py:124
  297.8 1.3 slice.39
  301.9 4.8 %slice.40 = f32[64,16,1024]{2,1,0:T(8,128)} slice(f32[64,16,1280]{2,1,0:T(8,128)} %all-to-all-done.2), slice={[0:64], [0:16], [0:1024]} | slice | bytes 8388608 | tf_op jit(solution)/shard_map/slice | solution.py:137
  306.7 2.9 gather_fusion.1
  309.6 6.2 %fusion.1 = bf16[512,1024]{1,0:T(8,128)(2,1)} fusion(f32[32,16,1024]{2,1,0:T(8,128)S(1)} %gather_fusion.1, bf16[512,2048]{1,0:T(8,128)(2,1)} %all-gather.2.cloned.1.call-done, bf16[1024,2048]{1,0:T(8,128)(2,1)} %param.11, pred[512]{0:T(512)(128)(4,1)S(1)} %broadcast_in_dim.123), kind=kOutput, calls=%fused_computation.7 | convolution fusion | flops 2149056512 | bytes 9437696 | tf_op jit(solution)/shard_map/dot_general | solution.py:143
  (69 shorter events, 11.5 us)
Async XLA Ops:
  7.2 120.2 %copy-start = (bf16[8,1024,64]{1,2,0:T(8,128)(2,1)S(1)}, bf16[8,1024,64]{1,2,0:T(8,128)(2,1)}, u32[]{:S(2)}) copy-start(bf16[8,1024,64]{1,2,0:T(8,128)(2,1)} %param.12) | copy-start | bytes 3145732
  8.1 0.8 copy-start.8
  8.3 0.5 copy-start.10
  10.6 12.2 %copy-start.1 = (bf16[512,1024]{1,0:T(8,128)(2,1)S(1)}, bf16[512,1024]{1,0:T(8,128)(2,1)}, u32[]{:S(2)}) copy-start(bf16[512,1024]{1,0:T(8,128)(2,1)} %param.10) | copy-start | bytes 3145732
  11.7 32.6 %all-to-all-start = ((bf16[64,16,384]{2,1,0:T(8,128)(2,1)}), bf16[64,16,384]{2,1,0:T(8,128)(2,1)}, u32[]{:S(2)}, u32[]{:S(2)}) async-start(bf16[64,16,384]{2,1,0:T(8,128)(2,1)} %fusion.19), calls=%async_computation.1 | async-start | bytes 1572864 | tf_op jit(solution)/shard_map/all_to_all | solution.py:66
  46.7 83.9 %all-to-all-start.1 = ((bf16[64,16,1024]{2,1,0:T(8,128)(2,1)}), bf16[64,16,1024]{2,1,0:T(8,128)(2,1)S(1)}, u32[]{:S(2)}, u32[]{:S(2)}) async-start(bf16[64,16,1024]{2,1,0:T(8,128)(2,1)} %bitcast.28), calls=%async_computation.2 | async-start | bytes 4194304 | tf_op jit(solution)/shard_map/all_to_all | solution.py:68
  52.2 74.2 %all-reduce.4.cloned.1.call-start = ((), (), s32[]{:S(2)}) async-start(), calls=%async_computation.5 | async-start | bytes 524288 | tf_op jit(solution)/shard_map/psum | solution.py:105
  58.9 241.0 %reduce-scatter.2.cloned.1.call-start = ((), (), s32[]{:S(2)}) async-start(), calls=%async_computation.4 | async-start | bytes 4718592 | tf_op jit(solution)/shard_map/reduce_scatter | solution.py:31
  65.9 0.7 copy-start.6
  65.9 0.7 copy-start.7
  67.6 63.0 %copy-start.4 = (bf16[1024,8]{0,1:T(8,128)(2,1)}, bf16[1024,8]{0,1:T(8,128)(2,1)S(1)}, u32[]{:S(2)}) copy-start(bf16[1024,8]{0,1:T(8,128)(2,1)S(1)} %convert_element_type.81) | copy-start | bytes 49156
  127.4 3.2 %copy-start.2 = (bf16[1024,64]{0,1:T(8,128)(2,1)}, bf16[1024,64]{0,1:T(8,128)(2,1)S(1)}, u32[]{:S(2)}) copy-start(bf16[1024,64]{0,1:T(8,128)(2,1)S(1)} %multiply_convert_fusion) | copy-start | bytes 393220
  166.5 10.7 %copy-start.9 = (s32[32]{0:T(128)S(1)}, s32[32]{0:T(128)}, u32[]{:S(2)}) copy-start(s32[32]{0:T(128)} %copy-done.8) | copy-start | bytes 388
  166.5 10.7 %copy-start.11 = (s32[32]{0:T(128)S(1)}, s32[32]{0:T(128)}, u32[]{:S(2)}) copy-start(s32[32]{0:T(128)} %copy-done.10) | copy-start | bytes 388
  166.5 10.7 %copy-start.5 = (bf16[1024,8]{0,1:T(8,128)(2,1)S(1)}, bf16[1024,8]{0,1:T(8,128)(2,1)}, u32[]{:S(2)}) copy-start(bf16[1024,8]{0,1:T(8,128)(2,1)} %copy-done.4) | copy-start | bytes 49156
  166.5 131.3 %all-to-all-start.2 = ((f32[64,16,1280]{2,1,0:T(8,128)}), f32[64,16,1280]{2,1,0:T(8,128)}, u32[]{:S(2)}, u32[]{:S(2)}) async-start(f32[64,16,1280]{2,1,0:T(8,128)} %pad_maximum_fusion), calls=%async_computation.3 | async-start | bytes 10485760 | tf_op jit(solution)/shard_map/all_to_all | solution.py:124
  176.3 3.3 %copy-start.3 = (bf16[1024,64]{0,1:T(8,128)(2,1)S(1)}, bf16[1024,64]{0,1:T(8,128)(2,1)}, u32[]{:S(2)}) copy-start(bf16[1024,64]{0,1:T(8,128)(2,1)} %copy-done.2) | copy-start | bytes 393220
  176.3 133.3 %all-gather.2.cloned.1.call-start = ((), (), s32[]{:S(2)}) async-start(), calls=%async_computation.6 | async-start | bytes 2359296 | tf_op jit(solution)/shard_map/all_gather | solution.py:144
Sparse Core Ops, SparseCore 0:
  59.0 67.3 all-reduce.3
  128.9 40.7 reduce-scatter.1
  178.9 30.4 all-gather.1

commit v7 on v5

--- a/solution.py
+++ b/solution.py
@@ -58,12 +58,7 @@
         preferred_element_type=jnp.float32,
     ).astype(jnp.bfloat16)
     slot_adapter = jnp.sum(jnp.where(placement, local_index[None, :] + 1, 0), axis=1) - 1
-    tag = jnp.zeros((storage_position_count, BLOCK_TOKENS, 128), jnp.bfloat16)
-    tag = tag.at[:, 0, 0].set((slot_adapter + 1).astype(jnp.bfloat16))
-    tagged_grads = jnp.concatenate(
-        [send_grads.reshape(storage_position_count, BLOCK_TOKENS, column_portion), tag], axis=2
-    )
-    arrived_rows, arrived_tagged = (
+    arrived_rows, arrived_grads, arrived_adapter = (
         lax.all_to_all(
             send_rows.reshape(storage_position_count, BLOCK_TOKENS, width_portion),
             "tok",
@@ -71,10 +66,15 @@
             concat_axis=0,
             tiled=True,
         ),
-        lax.all_to_all(tagged_grads, "tok", split_axis=0, concat_axis=0, tiled=True),
+        lax.all_to_all(
+            send_grads.reshape(storage_position_count, BLOCK_TOKENS, column_portion),
+            "tok",
+            split_axis=0,
+            concat_axis=0,
+            tiled=True,
+        ),
+        lax.all_to_all(slot_adapter, "tok", split_axis=0, concat_axis=0, tiled=True),
     )
-    arrived_grads = arrived_tagged[:, :, :column_portion]
-    arrived_adapter = arrived_tagged[:, 0, column_portion].astype(jnp.int32) - 1
     row_total = storage_position_count * BLOCK_TOKENS
     input_row_block = arrived_rows.reshape(row_total, width_portion)
     gradient_row_block = arrived_grads.reshape(row_total, column_portion)

time: 320 us -> 324 us (1.012)
  starting transfers between devices: 26.3 us -> 33 us
    all_to_all x1 -> x2, starting transfers between devices: 11 us -> 16.4 us  [the longest x1 11.1 us: per_device(): lax.all_to_all(slot_adapter, 'tok', split_axis=0, concat_axis=0, tiled=True)]
    all_to_all x1 -> x2, waiting for transfers between devices: 16.5 us -> 16 us  [the longest x1 10.8 us: per_device(): lax.all_to_all(send_grads.reshape(storage_position_count, BLOCK_TOKENS, c...]
  transfers between devices with their start and end apart: 6 -> 7, of which waited for: 3 -> 4; matrix products, arithmetic and copies ran while one was open for 15% -> 15% of each run, Pallas kernels for 0% -> 0%
where the time goes in v7:
time: 324 us; the launch traced here: 323 us
  waiting for transfers between devices  192 us (59%)
  starting transfers between devices  33 us (10%)
  blocking collectives  27.6 us (9%)
  matrix products  27.5 us (8%)
  local copies, waits for them, and re-layouts  19.2 us (6%)
  between operations  14.1 us (4%)
  other arithmetic  9.9 us (3%)
    all_to_all x1, waiting for transfers between devices, per_device(): lax.all_to_all(jnp.concatenate([adapter_output_rows.reshape(storage_posit...  116 us
    psum x1, waiting for transfers between devices, per_device(): low_sum, pull_sum = lax.psum((low_part, pull_part), 'tp')  58.9 us
    psum x1, blocking collectives, per_device(): low_sum, pull_sum = lax.psum((low_part, pull_part), 'tp')  27.6 us
    all_to_all x1, starting transfers between devices, per_device(): lax.all_to_all(slot_adapter, 'tok', split_axis=0, concat_axis=0, tiled=True)  11.1 us
    all_to_all x1, waiting for transfers between devices, per_device(): lax.all_to_all(send_grads.reshape(storage_position_count, BLOCK_TOKENS, c...  10.8 us
    all_to_all x1, starting transfers between devices, per_device(): lax.all_to_all(jnp.concatenate([adapter_output_rows.reshape(storage_posit...  9.94 us
    dot_general x1, matrix products, per_device(): lax.dot_general(weight_cols, tokens, (((0,), (1,)), ((), ())), preferred_...  6.97 us
    all_to_all x1, starting transfers between devices, per_device(): lax.all_to_all(send_rows.reshape(storage_position_count, BLOCK_TOKENS, wi...  6.54 us
  transfers between devices with their start and end apart: 7, of which 4 were waited for; matrix products, arithmetic and copies ran while one was open for 15% of the time, Pallas kernels for 0%

profile of v7, /device:TPU:27, one launch (start us, length us, event | category | flops | bytes accessed | tf_op | source)
XLA Modules:
  0.0 323.0 jit_solution(17419059075813431136)
XLA Ops:
  9.7 11.1 %all-to-all-start = ((s32[32,2,1]{1,2,0:T(1,128)}), s32[32,2,1]{1,2,0:T(1,128)S(1)}, u32[]{:S(2)}, u32[]{:S(2)}) async-start(s32[32,2,1]{1,2,0:T(1,128)} %bitcast.1), calls=%async_computation.1 | async-start | bytes 32768 | tf_op jit(solution)/shard_map/all_to_all | solution.py:76
  20.8 1.1 reshape.240
  23.2 5.2 %all-to-all-done = s32[32,2,1]{1,2,0:T(1,128)S(1)} async-done(((s32[32,2,1]{1,2,0:T(1,128)}), s32[32,2,1]{1,2,0:T(1,128)S(1)}, u32[]{:S(2)}, u32[]{:S(2)}) %all-to-all-start) | async-done | bytes 288 | tf_op jit(solution)/shard_map/all_to_all | solution.py:76
  28.4 5.4 %all-to-all-start.1 = ((bf16[64,16,256]{2,1,0:T(8,128)(2,1)}), bf16[64,16,256]{2,1,0:T(8,128)(2,1)}, u32[]{:S(2)}, u32[]{:S(2)}) async-start(bf16[64,16,256]{2,1,0:T(8,128)(2,1)} %bitcast.25), calls=%async_computation.2 | async-start | bytes 1048576 | tf_op jit(solution)/shard_map/all_to_all | solution.py:69
  35.1 2.5 copy.27
  37.7 10.8 %all-to-all-done.1 = bf16[64,16,256]{2,1,0:T(8,128)(2,1)} async-done(((bf16[64,16,256]{2,1,0:T(8,128)(2,1)}), bf16[64,16,256]{2,1,0:T(8,128)(2,1)}, u32[]{:S(2)}, u32[]{:S(2)}) %all-to-all-start.1) | async-done | bytes 524320 | tf_op jit(solution)/shard_map/all_to_all | solution.py:69
  48.5 6.5 %all-to-all-start.2 = ((bf16[64,16,1024]{2,1,0:T(8,128)(2,1)}), bf16[64,16,1024]{2,1,0:T(8,128)(2,1)S(1)}, u32[]{:S(2)}, u32[]{:S(2)}) async-start(bf16[64,16,1024]{2,1,0:T(8,128)(2,1)} %bitcast.28), calls=%async_computation.3 | async-start | bytes 4194304 | tf_op jit(solution)/shard_map/all_to_all | solution.py:62
  56.7 2.3 multiply_reduce_fusion.1
  59.1 7.0 %fusion.34 = f32[2048,512]{1,0:T(8,128)} fusion(bf16[1024,2048]{1,0:T(8,128)(2,1)} %param.9, bf16[512,1024]{1,0:T(8,128)(2,1)} %param.8), kind=kOutput, calls=%fused_computation.70 | convolution fusion | flops 2147483648 | bytes 9437184 | tf_op jit(solution)/shard_map/dot_general | solution.py:32
  67.8 58.9 %all-reduce.3.cloned.1.call-done = f32[1024,64]{0,1:T(8,128)} async-done(((f32[1024,64]{0,1:T(8,128)}), f32[1024,64]{0,1:T(8,128)}) %all-reduce.3.cloned.1.call-update) | async-done | bytes 262160 | tf_op jit(solution)/shard_map/psum | solution.py:106
  127.7 3.2 fusion.7
  130.9 1.3 fusion.35
  132.4 27.6 %all-reduce.4 = bf16[1024,64]{0,1:T(8,128)(2,1)S(1)} all-reduce(f32[1024,64]{0,1:T(8,128)S(1)} %multiply_reduce_fusion), channel_id=1, replica_groups=mesh['tok'=32,'tp'=8] {'tp'}, use_global_device_ids=true, to_apply=%region_10.11 | all-reduce | flops 65536 | bytes 393216 | tf_op jit(solution)/shard_map/psum | solution.py:106
  160.1 1.5 fusion.12
  161.6 5.1 %pad_maximum_fusion = f32[64,16,1280]{2,1,0:T(8,128)} fusion(f32[64,16,256]{2,1,0:T(8,128)S(1)} %bitcast.79, f32[64,16,1024]{2,1,0:T(8,128)} %bitcast.73), kind=kLoop, calls=%fused_computation.3 | loop fusion | flops 1310720 | bytes 10485760 | tf_op jit(solution)/shard_map/concatenate | solution.py:126
  166.7 9.9 %all-to-all-start.3 = ((f32[64,16,1280]{2,1,0:T(8,128)}), f32[64,16,1280]{2,1,0:T(8,128)}, u32[]{:S(2)}, u32[]{:S(2)}) async-start(f32[64,16,1280]{2,1,0:T(8,128)} %pad_maximum_fusion), calls=%async_computation.4 | async-start | bytes 10485760 | tf_op jit(solution)/shard_map/all_to_all | solution.py:125
  177.7 2.3 fusion.15
  179.9 2.6 convolution_bitcast_fusion
  182.5 116.0 %all-to-all-done.3 = f32[64,16,1280]{2,1,0:T(8,128)} async-done(((f32[64,16,1280]{2,1,0:T(8,128)}), f32[64,16,1280]{2,1,0:T(8,128)}, u32[]{:S(2)}, u32[]{:S(2)}) %all-to-all-start.3) | async-done | bytes 5242912 | tf_op jit(solution)/shard_map/all_to_all | solution.py:125
  298.5 1.3 slice.12
  300.6 1.1 fusion.18
  302.6 4.8 %slice.13 = f32[64,16,1024]{2,1,0:T(8,128)} slice(f32[64,16,1280]{2,1,0:T(8,128)} %all-to-all-done.3), slice={[0:64], [0:16], [0:1024]} | slice | bytes 8388608 | tf_op jit(solution)/shard_map/slice | solution.py:138
  307.4 2.9 gather_fusion.1
  310.3 6.2 %fusion.1 = bf16[512,1024]{1,0:T(8,128)(2,1)} fusion(f32[32,16,1024]{2,1,0:T(8,128)S(1)} %gather_fusion.1, bf16[512,2048]{1,0:T(8,128)(2,1)} %all-gather.2.cloned.1.call-done, bf16[1024,2048]{1,0:T(8,128)(2,1)} %param.9, pred[512]{0:T(512)(128)(4,1)S(1)} %broadcast_in_dim.122), kind=kOutput, calls=%fused_computation.7 | convolution fusion | flops 2149056512 | bytes 9437696 | tf_op jit(solution)/shard_map/dot_general | solution.py:144
  (71 shorter events, 12.4 us)
Async XLA Ops:
  7.2 120.5 %copy-start = (bf16[8,1024,64]{1,2,0:T(8,128)(2,1)S(1)}, bf16[8,1024,64]{1,2,0:T(8,128)(2,1)}, u32[]{:S(2)}) copy-start(bf16[8,1024,64]{1,2,0:T(8,128)(2,1)} %param.10) | copy-start | bytes 3145732
  7.2 26.6 %copy-start.1 = (bf16[512,1024]{1,0:T(8,128)(2,1)S(1)}, bf16[512,1024]{1,0:T(8,128)(2,1)}, u32[]{:S(2)}) copy-start(bf16[512,1024]{1,0:T(8,128)(2,1)} %param.8) | copy-start | bytes 3145732
  8.2 0.5 copy-start.8
  8.4 0.5 copy-start.10
  9.7 18.7 %all-to-all-start = ((s32[32,2,1]{1,2,0:T(1,128)}), s32[32,2,1]{1,2,0:T(1,128)S(1)}, u32[]{:S(2)}, u32[]{:S(2)}) async-start(s32[32,2,1]{1,2,0:T(1,128)} %bitcast.1), calls=%async_computation.1 | async-start | bytes 32768 | tf_op jit(solution)/shard_map/all_to_all | solution.py:76
  28.4 20.1 %all-to-all-start.1 = ((bf16[64,16,256]{2,1,0:T(8,128)(2,1)}), bf16[64,16,256]{2,1,0:T(8,128)(2,1)}, u32[]{:S(2)}, u32[]{:S(2)}) async-start(bf16[64,16,256]{2,1,0:T(8,128)(2,1)} %bitcast.25), calls=%async_computation.2 | async-start | bytes 1048576 | tf_op jit(solution)/shard_map/all_to_all | solution.py:69
  48.5 82.4 %all-to-all-start.2 = ((bf16[64,16,1024]{2,1,0:T(8,128)(2,1)}), bf16[64,16,1024]{2,1,0:T(8,128)(2,1)S(1)}, u32[]{:S(2)}, u32[]{:S(2)}) async-start(bf16[64,16,1024]{2,1,0:T(8,128)(2,1)} %bitcast.28), calls=%async_computation.3 | async-start | bytes 4194304 | tf_op jit(solution)/shard_map/all_to_all | solution.py:62
  55.0 71.6 %all-reduce.3.cloned.1.call-start = ((), (), s32[]{:S(2)}) async-start(), calls=%async_computation.6 | async-start | bytes 524288 | tf_op jit(solution)/shard_map/psum | solution.py:106
  59.0 241.6 %reduce-scatter.2.cloned.1.call-start = ((), (), s32[]{:S(2)}) async-start(), calls=%async_computation.5 | async-start | bytes 4718592 | tf_op jit(solution)/shard_map/reduce_scatter | solution.py:31
  66.1 0.7 copy-start.6
  66.1 0.7 copy-start.7
  67.8 63.1 %copy-start.4 = (bf16[1024,8]{0,1:T(8,128)(2,1)}, bf16[1024,8]{0,1:T(8,128)(2,1)S(1)}, u32[]{:S(2)}) copy-start(bf16[1024,8]{0,1:T(8,128)(2,1)S(1)} %convert_element_type.57) | copy-start | bytes 49156
  127.7 3.2 copy-start.2
  166.7 10.9 %copy-start.9 = (s32[32]{0:T(128)S(1)}, s32[32]{0:T(128)}, u32[]{:S(2)}) copy-start(s32[32]{0:T(128)} %copy-done.8) | copy-start | bytes 388
  166.7 10.9 %copy-start.11 = (s32[32]{0:T(128)S(1)}, s32[32]{0:T(128)}, u32[]{:S(2)}) copy-start(s32[32]{0:T(128)} %copy-done.10) | copy-start | bytes 388
  166.7 10.9 %copy-start.5 = (bf16[1024,8]{0,1:T(8,128)(2,1)S(1)}, bf16[1024,8]{0,1:T(8,128)(2,1)}, u32[]{:S(2)}) copy-start(bf16[1024,8]{0,1:T(8,128)(2,1)} %copy-done.4) | copy-start | bytes 49156
  166.7 131.8 %all-to-all-start.3 = ((f32[64,16,1280]{2,1,0:T(8,128)}), f32[64,16,1280]{2,1,0:T(8,128)}, u32[]{:S(2)}, u32[]{:S(2)}) async-start(f32[64,16,1280]{2,1,0:T(8,128)} %pad_maximum_fusion), calls=%async_computation.4 | async-start | bytes 10485760 | tf_op jit(solution)/shard_map/all_to_all | solution.py:125
  176.7 3.3 %copy-start.3 = (bf16[1024,64]{0,1:T(8,128)(2,1)S(1)}, bf16[1024,64]{0,1:T(8,128)(2,1)}, u32[]{:S(2)}) copy-start(bf16[1024,64]{0,1:T(8,128)(2,1)} %copy-done.2) | copy-start | bytes 393220
  176.7 133.6 %all-gather.2.cloned.1.call-start = ((), (), s32[]{:S(2)}) async-start(), calls=%async_computation.7 | async-start | bytes 2359296 | tf_op jit(solution)/shard_map/all_gather | solution.py:145
Sparse Core Ops, SparseCore 0:
  59.2 67.4 all-reduce.2
  129.2 40.7 reduce-scatter.1
  179.3 30.3 all-gather.1

commit v8 on v6

--- a/solution.py
+++ b/solution.py
@@ -121,21 +121,22 @@
     adapter_output_rows = jnp.einsum(
         "ymf,mcf->yc", gradient_picked, adapter_down_matrices, preferred_element_type=jnp.float32
     )
-    returned = lax.all_to_all(
-        jnp.concatenate(
-            [
-                adapter_output_rows.reshape(storage_position_count, BLOCK_TOKENS, width_portion),
-                adapter_increment.reshape(storage_position_count, BLOCK_TOKENS, column_portion),
-            ],
-            axis=2,
+    delta_back, row_input_gradient = (
+        lax.all_to_all(
+            adapter_increment.reshape(storage_position_count, BLOCK_TOKENS, column_portion),
+            "tok",
+            split_axis=0,
+            concat_axis=0,
+            tiled=True,
         ),
-        "tok",
-        split_axis=0,
-        concat_axis=0,
-        tiled=True,
+        lax.all_to_all(
+            adapter_output_rows.reshape(storage_position_count, BLOCK_TOKENS, width_portion),
+            "tok",
+            split_axis=0,
+            concat_axis=0,
+            tiled=True,
+        ),
     )
-    row_input_gradient = returned[:, :, :width_portion]
-    delta_back = returned[:, :, width_portion:]
     adapter_input_gradient = jnp.take(row_input_gradient, destination, axis=0)
     mine_delta = jnp.take(delta_back, destination, axis=0)
     projected = (base_out + mine_delta.reshape(token_rows, column_portion)).astype(jnp.bfloat16)

time: 324 us -> 280 us (0.86)
  waiting for transfers between devices: 193 us -> 160 us
  local copies, waits for them, and re-layouts: 19.9 us -> 13.3 us
  other arithmetic: 12.2 us -> 7.16 us
    psum x1, waiting for transfers between devices: 58.8 us -> 0.02 us  [per_device(): low_sum, pull_sum = lax.psum((low_part, pull_part), 'tp')]
    all_to_all x1, waiting for transfers between devices: 0.01 us -> 32.2 us  [per_device(): lax.all_to_all(send_rows.reshape(storage_position_count, BLOCK_TOKENS, wi...]
    all_to_all x1 -> x2, waiting for transfers between devices: 116 us -> 108 us  [the longest x1 84.7 us: per_device(): lax.all_to_all(adapter_output_rows.reshape(storage_position_count, BLOCK_...]
    slice x2 -> x0, local copies, waits for them, and re-layouts: 6.08 us -> none  [the longest x1 4.79 us: per_device(): row_input_gradient = returned[:, :, :width_portion]]
    concatenate x1 -> x0, other arithmetic: 5.1 us -> none  [per_device(): jnp.concatenate([adapter_output_rows.reshape(storage_position_count, BLOC...]
    all_to_all x1 -> x2, starting transfers between devices: 9.76 us -> 11.7 us  [the longest x1 6.42 us: per_device(): lax.all_to_all(adapter_increment.reshape(storage_position_count, BLOCK_TO...]
  transfers between devices with their start and end apart: 6 -> 7, of which waited for: 3 -> 4; matrix products, arithmetic and copies ran while one was open for 15% -> 13% of each run, Pallas kernels for 0% -> 0%
where the time goes in v8:
time: 280 us; the launch traced here: 278 us
  waiting for transfers between devices  160 us (57%)
  matrix products  29.1 us (10%)
  starting transfers between devices  28.4 us (10%)
  blocking collectives  26.9 us (10%)
  between operations  14 us (5%)
  local copies, waits for them, and re-layouts  13.3 us (5%)
  other arithmetic  7.16 us (3%)
    all_to_all x1, waiting for transfers between devices, per_device(): lax.all_to_all(adapter_output_rows.reshape(storage_position_count, BLOCK_...  84.7 us
    all_to_all x1, waiting for transfers between devices, per_device(): lax.all_to_all(send_rows.reshape(storage_position_count, BLOCK_TOKENS, wi...  32.2 us
    psum x1, blocking collectives, per_device(): low_sum, pull_sum = lax.psum((low_part, pull_part), 'tp')  26.9 us
    all_to_all x1, waiting for transfers between devices, per_device(): lax.all_to_all(adapter_increment.reshape(storage_position_count, BLOCK_TO...  23.8 us
    all_to_all x1, waiting for transfers between devices, per_device(): lax.all_to_all(tagged_grads, 'tok', split_axis=0, concat_axis=0, tiled=True)  18.1 us
    all_to_all x1, starting transfers between devices, per_device(): lax.all_to_all(tagged_grads, 'tok', split_axis=0, concat_axis=0, tiled=True)  11.1 us
    dot_general x1, matrix products, per_device(): lax.dot_general(weight_cols, tokens, (((0,), (1,)), ((), ())), preferred_...  6.81 us
    all_to_all x1, starting transfers between devices, per_device(): lax.all_to_all(adapter_increment.reshape(storage_position_count, BLOCK_TO...  6.42 us
  transfers between devices with their start and end apart: 7, of which 4 were waited for; matrix products, arithmetic and copies ran while one was open for 13% of the time, Pallas kernels for 0%

profile of v8, /device:TPU:27, one launch (start us, length us, event | category | flops | bytes accessed | tf_op | source)
XLA Modules:
  0.0 278.4 jit_solution(11248990414518391411)
XLA Ops:
  11.2 11.1 %all-to-all-start = ((bf16[64,16,384]{2,1,0:T(8,128)(2,1)}), bf16[64,16,384]{2,1,0:T(8,128)(2,1)}, u32[]{:S(2)}, u32[]{:S(2)}) async-start(bf16[64,16,384]{2,1,0:T(8,128)(2,1)} %fusion.19), calls=%async_computation.1 | async-start | bytes 1572864 | tf_op jit(solution)/shard_map/all_to_all | solution.py:66
  22.3 1.3 reshape.268
  23.6 2.0 convolution_convert_fusion
  25.6 18.1 %all-to-all-done = bf16[64,16,384]{2,1,0:T(8,128)(2,1)} async-done(((bf16[64,16,384]{2,1,0:T(8,128)(2,1)}), bf16[64,16,384]{2,1,0:T(8,128)(2,1)}, u32[]{:S(2)}, u32[]{:S(2)}) %all-to-all-start) | async-done | bytes 786464 | tf_op jit(solution)/shard_map/all_to_all | solution.py:66
  43.7 2.5 copy.36
  46.2 5.5 %all-to-all-start.1 = ((bf16[64,16,1024]{2,1,0:T(8,128)(2,1)}), bf16[64,16,1024]{2,1,0:T(8,128)(2,1)S(1)}, u32[]{:S(2)}, u32[]{:S(2)}) async-start(bf16[64,16,1024]{2,1,0:T(8,128)(2,1)} %bitcast.27), calls=%async_computation.2 | async-start | bytes 4194304 | tf_op jit(solution)/shard_map/all_to_all | solution.py:68
  51.8 1.9 slice.26
  53.6 2.1 add_reduce_fusion
  56.1 2.3 multiply_reduce_fusion
  58.4 6.8 %fusion.36 = f32[2048,512]{1,0:T(8,128)} fusion(bf16[1024,2048]{1,0:T(8,128)(2,1)} %param.11, bf16[512,1024]{1,0:T(8,128)(2,1)} %param.10), kind=kOutput, calls=%fused_computation.73 | convolution fusion | flops 2147483648 | bytes 9437184 | tf_op jit(solution)/shard_map/dot_general | solution.py:32
  67.0 32.2 %all-to-all-done.1 = bf16[64,16,1024]{2,1,0:T(8,128)(2,1)S(1)} async-done(((bf16[64,16,1024]{2,1,0:T(8,128)(2,1)}), bf16[64,16,1024]{2,1,0:T(8,128)(2,1)S(1)}, u32[]{:S(2)}, u32[]{:S(2)}) %all-to-all-start.1) | async-done | bytes 2097184 | tf_op jit(solution)/shard_map/all_to_all | solution.py:68
  99.2 1.3 fusion.37
  100.8 26.9 %all-reduce.5 = bf16[1024,64]{0,1:T(8,128)(2,1)S(1)} all-reduce(f32[1024,64]{0,1:T(8,128)S(1)} %multiply_reduce_fusion.1), channel_id=1, replica_groups=mesh['tok'=32,'tp'=8] {'tp'}, use_global_device_ids=true, to_apply=%region_8.9 | all-reduce | flops 65536 | bytes 393216 | tf_op jit(solution)/shard_map/psum | solution.py:105
  127.7 1.5 fusion.13
  129.2 6.4 %all-to-all-start.2 = ((f32[64,16,256]{2,1,0:T(8,128)}), f32[64,16,256]{2,1,0:T(8,128)S(1)}, u32[]{:S(2)}, u32[]{:S(2)}) async-start(f32[64,16,256]{2,1,0:T(8,128)} %bitcast.7), calls=%async_computation.3 | async-start | bytes 2097152 | tf_op jit(solution)/shard_map/all_to_all | solution.py:125
  136.6 3.3 %fusion.4 = f32[1024,1024,1]{1,0,2:T(8,128)} fusion(bf16[8,1024,64]{1,2,0:T(8,128)(2,1)S(1)} %copy-done, bf16[1024,64]{0,1:T(8,128)(2,1)S(1)} %multiply_convert_fusion, bf16[1024,8]{0,1:T(8,128)(2,1)S(1)} %convert_element_type.82), kind=kOutput, calls=%fused_computation.13 | convolution fusion | flops 1074266112 | bytes 5390336 | tf_op jit(solution)/shard_map/ymf,mcf->yc/dot_general | solution.py:121
  139.9 23.8 %all-to-all-done.2 = f32[64,16,256]{2,1,0:T(8,128)S(1)} async-done(((f32[64,16,256]{2,1,0:T(8,128)}), f32[64,16,256]{2,1,0:T(8,128)S(1)}, u32[]{:S(2)}, u32[]{:S(2)}) %all-to-all-start.2) | async-done | bytes 1048608 | tf_op jit(solution)/shard_map/all_to_all | solution.py:125
  163.6 5.3 %all-to-all-start.3 = ((f32[64,16,1024]{2,1,0:T(8,128)}), f32[64,16,1024]{2,1,0:T(8,128)}, u32[]{:S(2)}, u32[]{:S(2)}) async-start(f32[64,16,1024]{2,1,0:T(8,128)} %bitcast.73), calls=%async_computation.4 | async-start | bytes 8388608 | tf_op jit(solution)/shard_map/all_to_all | solution.py:132
  169.9 1.2 fusion.16
  171.1 4.2 %convolution_bitcast_fusion = f32[8,1024,64]{1,2,0:T(8,128)} fusion(bf16[1024,1024,1]{1,0,2:T(8,128)(2,1)} %bitcast.76, bf16[1024,64]{0,1:T(8,128)(2,1)S(1)} %multiply_convert_fusion, bf16[1024,8]{0,1:T(8,128)(2,1)S(1)} %convert_element_type.82), kind=kOutput, calls=%fused_computation.9 | convolution fusion | flops 1074266112 | bytes 4341760 | tf_op jit(solution)/shard_map/rd,rak->adk/dot_general | solution.py:115
  176.1 1.1 fusion.20
  178.1 84.7 %all-to-all-done.3 = f32[64,16,1024]{2,1,0:T(8,128)} async-done(((f32[64,16,1024]{2,1,0:T(8,128)}), f32[64,16,1024]{2,1,0:T(8,128)}, u32[]{:S(2)}, u32[]{:S(2)}) %all-to-all-start.3) | async-done | bytes 4194336 | tf_op jit(solution)/shard_map/all_to_all | solution.py:132
  262.8 2.9 %gather_fusion.1 = f32[32,16,1024]{2,1,0:T(8,128)S(1)} fusion(f32[64,16,1024]{2,1,0:T(8,128)} %all-to-all-done.3, s32[1024]{0:T(1024)S(1)} %pad_clamp_fusion), kind=kCustom, calls=%fused_computation.1 | custom fusion | bytes 4194432 | tf_op jit(solution)/shard_map/jit(_take)/gather | solution.py:140
  265.7 6.2 %fusion.1 = bf16[512,1024]{1,0:T(8,128)(2,1)} fusion(f32[32,16,1024]{2,1,0:T(8,128)S(1)} %gather_fusion.1, bf16[512,2048]{1,0:T(8,128)(2,1)} %all-gather.2.cloned.1.call-done, bf16[1024,2048]{1,0:T(8,128)(2,1)} %param.11, pred[512]{0:T(512)(128)(4,1)S(1)} %broadcast_in_dim.123), kind=kOutput, calls=%fused_computation.6 | convolution fusion | flops 2149056512 | bytes 9437696 | tf_op jit(solution)/shard_map/dot_general | solution.py:144
  (58 shorter events, 9.9 us)
Async XLA Ops:
  7.2 92.0 %copy-start = (bf16[8,1024,64]{1,2,0:T(8,128)(2,1)S(1)}, bf16[8,1024,64]{1,2,0:T(8,128)(2,1)}, u32[]{:S(2)}) copy-start(bf16[8,1024,64]{1,2,0:T(8,128)(2,1)} %param.12) | copy-start | bytes 3145732
  10.1 12.2 %copy-start.2 = (bf16[512,1024]{1,0:T(8,128)(2,1)S(1)}, bf16[512,1024]{1,0:T(8,128)(2,1)}, u32[]{:S(2)}) copy-start(bf16[512,1024]{1,0:T(8,128)(2,1)} %param.10) | copy-start | bytes 3145732
  11.2 32.6 %all-to-all-start = ((bf16[64,16,384]{2,1,0:T(8,128)(2,1)}), bf16[64,16,384]{2,1,0:T(8,128)(2,1)}, u32[]{:S(2)}, u32[]{:S(2)}) async-start(bf16[64,16,384]{2,1,0:T(8,128)(2,1)} %fusion.19), calls=%async_computation.1 | async-start | bytes 1572864 | tf_op jit(solution)/shard_map/all_to_all | solution.py:66
  46.2 52.9 %all-to-all-start.1 = ((bf16[64,16,1024]{2,1,0:T(8,128)(2,1)}), bf16[64,16,1024]{2,1,0:T(8,128)(2,1)S(1)}, u32[]{:S(2)}, u32[]{:S(2)}) async-start(bf16[64,16,1024]{2,1,0:T(8,128)(2,1)} %bitcast.27), calls=%async_computation.2 | async-start | bytes 4194304 | tf_op jit(solution)/shard_map/all_to_all | solution.py:68
  51.7 83.9 %all-reduce.4.cloned.1.call-start = ((), (), s32[]{:S(2)}) async-start(), calls=%async_computation.7 | async-start | bytes 524288 | tf_op jit(solution)/shard_map/psum | solution.py:105
  58.4 117.7 %reduce-scatter.2.cloned.1.call-start = ((), (), s32[]{:S(2)}) async-start(), calls=%async_computation.5 | async-start | bytes 4718592 | tf_op jit(solution)/shard_map/reduce_scatter | solution.py:31
  65.3 0.7 copy-start.4
  65.3 0.7 copy-start.5
  99.2 1.3 copy-start.1
  100.5 27.2 %copy-start.6 = (bf16[8,64,256]{2,1,0:T(8,128)(2,1)S(1)}, bf16[8,64,256]{2,1,0:T(8,128)(2,1)}, u32[]{:S(2)}) copy-start(bf16[8,64,256]{2,1,0:T(8,128)(2,1)} %param.13) | copy-start | bytes 786436
  129.2 34.5 %all-to-all-start.2 = ((f32[64,16,256]{2,1,0:T(8,128)}), f32[64,16,256]{2,1,0:T(8,128)S(1)}, u32[]{:S(2)}, u32[]{:S(2)}) async-start(f32[64,16,256]{2,1,0:T(8,128)} %bitcast.7), calls=%async_computation.3 | async-start | bytes 2097152 | tf_op jit(solution)/shard_map/all_to_all | solution.py:125
  163.6 6.2 %copy-start.3 = (bf16[64,16,256]{2,1,0:T(8,128)(2,1)S(1)}, bf16[64,16,256]{2,1,0:T(8,128)(2,1)}, u32[]{:S(2)}) copy-start(bf16[64,16,256]{2,1,0:T(8,128)(2,1)} %slice.26) | copy-start | bytes 1572868
  163.6 99.2 %all-to-all-start.3 = ((f32[64,16,1024]{2,1,0:T(8,128)}), f32[64,16,1024]{2,1,0:T(8,128)}, u32[]{:S(2)}, u32[]{:S(2)}) async-start(f32[64,16,1024]{2,1,0:T(8,128)} %bitcast.73), calls=%async_computation.4 | async-start | bytes 8388608 | tf_op jit(solution)/shard_map/all_to_all | solution.py:132
  168.9 96.8 %all-gather.2.cloned.1.call-start = ((), (), s32[]{:S(2)}) async-start(), calls=%async_computation.6 | async-start | bytes 2359296 | tf_op jit(solution)/shard_map/all_gather | solution.py:145
Sparse Core Ops, SparseCore 0:
  58.5 67.4 all-reduce.3
  128.5 39.7 reduce-scatter.1
  171.6 30.7 all-gather.1

commit v9 on v8

--- a/solution.py
+++ b/solution.py
@@ -58,11 +58,9 @@
         preferred_element_type=jnp.float32,
     ).astype(jnp.bfloat16)
     slot_adapter = jnp.sum(jnp.where(placement, local_index[None, :] + 1, 0), axis=1) - 1
-    tag = jnp.zeros((storage_position_count, BLOCK_TOKENS, 128), jnp.bfloat16)
-    tag = tag.at[:, 0, 0].set((slot_adapter + 1).astype(jnp.bfloat16))
-    tagged_grads = jnp.concatenate(
-        [send_grads.reshape(storage_position_count, BLOCK_TOKENS, column_portion), tag], axis=2
-    )
+    tag = jnp.zeros((storage_position_count, 128), jnp.bfloat16)
+    tag = tag.at[:, 0].set((slot_adapter + 1).astype(jnp.bfloat16))
+    tagged_grads = jnp.concatenate([send_grads, tag], axis=1)
     arrived_tagged = lax.all_to_all(tagged_grads, "tok", split_axis=0, concat_axis=0, tiled=True)
     send_rows, arrived_tagged = lax.optimization_barrier((send_rows, arrived_tagged))
     arrived_rows = lax.all_to_all(
@@ -72,8 +70,8 @@
         concat_axis=0,
         tiled=True,
     )
-    arrived_grads = arrived_tagged[:, :, :column_portion]
-    arrived_adapter = arrived_tagged[:, 0, column_portion].astype(jnp.int32) - 1
+    arrived_grads = arrived_tagged[:, : BLOCK_TOKENS * column_portion]
+    arrived_adapter = arrived_tagged[:, BLOCK_TOKENS * column_portion].astype(jnp.int32) - 1
     row_total = storage_position_count * BLOCK_TOKENS
     input_row_block = arrived_rows.reshape(row_total, width_portion)
     gradient_row_block = arrived_grads.reshape(row_total, column_portion)

time: 280 us -> 281 us (level)
    all_to_all x1, waiting for transfers between devices: 18.1 us -> 13.1 us  [per_device(): lax.all_to_all(tagged_grads, 'tok', split_axis=0, concat_axis=0, tiled=True)]
    all_to_all x1, waiting for transfers between devices: 32.2 us -> 37 us  [per_device(): lax.all_to_all(send_rows.reshape(storage_position_count, BLOCK_TOKENS, wi...]
    all_to_all x0 -> x2, local copies, waits for them, and re-layouts: none -> 3.05 us  [per_device(): lax.all_to_all(tagged_grads, 'tok', split_axis=0, concat_axis=0, tiled=True)]
  transfers between devices with their start and end apart: 7 -> 7, of which waited for: 4 -> 4; matrix products, arithmetic and copies ran while one was open for 13% -> 12% of each run, Pallas kernels for 0% -> 0%
where the time goes in v9:
time: 281 us; the launch traced here: 279 us
  waiting for transfers between devices  159 us (57%)
  matrix products  29.3 us (10%)
  starting transfers between devices  29.1 us (10%)
  blocking collectives  26.7 us (10%)
  local copies, waits for them, and re-layouts  14.8 us (5%)
  between operations  14.1 us (5%)
  other arithmetic  5.44 us (2%)
    all_to_all x1, waiting for transfers between devices, per_device(): lax.all_to_all(adapter_output_rows.reshape(storage_position_count, BLOCK_...  84.8 us
    all_to_all x1, waiting for transfers between devices, per_device(): lax.all_to_all(send_rows.reshape(storage_position_count, BLOCK_TOKENS, wi...  37 us
    psum x1, blocking collectives, per_device(): low_sum, pull_sum = lax.psum((low_part, pull_part), 'tp')  26.7 us
    all_to_all x1, waiting for transfers between devices, per_device(): lax.all_to_all(adapter_increment.reshape(storage_position_count, BLOCK_TO...  23.8 us
    all_to_all x1, waiting for transfers between devices, per_device(): lax.all_to_all(tagged_grads, 'tok', split_axis=0, concat_axis=0, tiled=True)  13.1 us
    all_to_all x1, starting transfers between devices, per_device(): lax.all_to_all(tagged_grads, 'tok', split_axis=0, concat_axis=0, tiled=True)  11.1 us
    all_to_all x1, starting transfers between devices, per_device(): lax.all_to_all(adapter_increment.reshape(storage_position_count, BLOCK_TO...  6.91 us
    dot_general x1, matrix products, per_device(): lax.dot_general(weight_cols, tokens, (((0,), (1,)), ((), ())), preferred_...  6.52 us
  transfers between devices with their start and end apart: 7, of which 4 were waited for; matrix products, arithmetic and copies ran while one was open for 12% of the time, Pallas kernels for 0%

profile of v9, /device:TPU:27, one launch (start us, length us, event | category | flops | bytes accessed | tf_op | source)
XLA Modules:
  0.0 278.9 jit_solution(2069753262458834740)
XLA Ops:
  9.8 1.1 reshape.262
  12.3 11.1 %all-to-all-start = ((bf16[32,2,4224]{2,1,0:T(2,128)(2,1)}), bf16[32,2,4224]{2,1,0:T(2,128)(2,1)}, u32[]{:S(2)}, u32[]{:S(2)}) async-start(bf16[32,2,4224]{2,1,0:T(2,128)(2,1)} %all_to_all.17), calls=%async_computation.1 | async-start | bytes 1081344 | tf_op jit(solution)/shard_map/all_to_all | solution.py:64
  23.4 1.3 reshape.261
  24.8 2.0 convolution_convert_fusion
  26.8 13.1 %all-to-all-done = bf16[32,2,4224]{2,1,0:T(2,128)(2,1)} async-done(((bf16[32,2,4224]{2,1,0:T(2,128)(2,1)}), bf16[32,2,4224]{2,1,0:T(2,128)(2,1)}, u32[]{:S(2)}, u32[]{:S(2)}) %all-to-all-start) | async-done | bytes 540704 | tf_op jit(solution)/shard_map/all_to_all | solution.py:64
  39.9 2.0 all_to_all.19
  41.9 2.5 copy.30
  44.4 5.7 %all-to-all-start.1 = ((bf16[64,16,1024]{2,1,0:T(8,128)(2,1)}), bf16[64,16,1024]{2,1,0:T(8,128)(2,1)}, u32[]{:S(2)}, u32[]{:S(2)}) async-start(bf16[64,16,1024]{2,1,0:T(8,128)(2,1)} %bitcast.22), calls=%async_computation.2 | async-start | bytes 4194304 | tf_op jit(solution)/shard_map/all_to_all | solution.py:66
  51.1 1.2 multiply_reduce_fusion
  52.4 6.5 %fusion.37 = f32[2048,512]{1,0:T(8,128)} fusion(bf16[1024,2048]{1,0:T(8,128)(2,1)} %param.11, bf16[512,1024]{1,0:T(8,128)(2,1)S(1)} %copy-done.3), kind=kOutput, calls=%fused_computation.75 | convolution fusion | flops 2147483648 | bytes 9437184 | tf_op jit(solution)/shard_map/dot_general | solution.py:32
  60.6 37.0 %all-to-all-done.1 = bf16[64,16,1024]{2,1,0:T(8,128)(2,1)} async-done(((bf16[64,16,1024]{2,1,0:T(8,128)(2,1)}), bf16[64,16,1024]{2,1,0:T(8,128)(2,1)}, u32[]{:S(2)}, u32[]{:S(2)}) %all-to-all-start.1) | async-done | bytes 2097184 | tf_op jit(solution)/shard_map/all_to_all | solution.py:66
  97.6 2.9 %fusion.38 = f32[1024,512]{0,1:S(1)} fusion(bf16[1024,1024]{1,0:T(8,128)(2,1)} %bitcast.2, bf16[1024,512]{0,1:T(8,128)(2,1)S(1)} %bitcast.66), kind=kOutput, calls=%fused_computation.76 | convolution fusion | flops 1073741824 | bytes 5242880
  100.8 26.7 %all-reduce.5 = bf16[1024,64]{0,1:T(8,128)(2,1)S(1)} all-reduce(f32[1024,64]{0,1:T(8,128)S(1)} %multiply_reduce_fusion.1), channel_id=1, replica_groups=mesh['tok'=32,'tp'=8] {'tp'}, use_global_device_ids=true, to_apply=%region_9.10 | all-reduce | flops 65536 | bytes 393216 | tf_op jit(solution)/shard_map/psum | solution.py:103
  127.5 1.5 fusion.12
  129.0 6.9 %all-to-all-start.2 = ((f32[64,16,256]{2,1,0:T(8,128)}), f32[64,16,256]{2,1,0:T(8,128)S(1)}, u32[]{:S(2)}, u32[]{:S(2)}) async-start(f32[64,16,256]{2,1,0:T(8,128)} %bitcast.7), calls=%async_computation.3 | async-start | bytes 2097152 | tf_op jit(solution)/shard_map/all_to_all | solution.py:123
  137.0 3.3 %fusion.3 = f32[1024,1024,1]{1,0,2:T(8,128)} fusion(bf16[8,1024,64]{1,2,0:T(8,128)(2,1)S(1)} %copy-done, bf16[1024,64]{0,1:T(8,128)(2,1)S(1)} %multiply_convert_fusion, bf16[1024,8]{0,1:T(8,128)(2,1)S(1)} %convert_element_type.75), kind=kOutput, calls=%fused_computation.11 | convolution fusion | flops 1074266112 | bytes 5390336 | tf_op jit(solution)/shard_map/ymf,mcf->yc/dot_general | solution.py:119
  140.2 23.8 %all-to-all-done.2 = f32[64,16,256]{2,1,0:T(8,128)S(1)} async-done(((f32[64,16,256]{2,1,0:T(8,128)}), f32[64,16,256]{2,1,0:T(8,128)S(1)}, u32[]{:S(2)}, u32[]{:S(2)}) %all-to-all-start.2) | async-done | bytes 1048608 | tf_op jit(solution)/shard_map/all_to_all | solution.py:123
  164.0 5.3 %all-to-all-start.3 = ((f32[64,16,1024]{2,1,0:T(8,128)}), f32[64,16,1024]{2,1,0:T(8,128)}, u32[]{:S(2)}, u32[]{:S(2)}) async-start(f32[64,16,1024]{2,1,0:T(8,128)} %bitcast.68), calls=%async_computation.4 | async-start | bytes 8388608 | tf_op jit(solution)/shard_map/all_to_all | solution.py:130
  170.3 1.2 fusion.15
  171.5 4.2 %convolution_bitcast_fusion = f32[8,1024,64]{1,2,0:T(8,128)} fusion(bf16[1024,1024,1]{1,0,2:T(8,128)(2,1)} %bitcast.15, bf16[1024,64]{0,1:T(8,128)(2,1)S(1)} %multiply_convert_fusion, bf16[1024,8]{0,1:T(8,128)(2,1)S(1)} %convert_element_type.75), kind=kOutput, calls=%fused_computation.9 | convolution fusion | flops 1074266112 | bytes 4341760 | tf_op jit(solution)/shard_map/rd,rak->adk/dot_general | solution.py:113
  176.5 1.1 fusion.20
  178.5 84.8 %all-to-all-done.3 = f32[64,16,1024]{2,1,0:T(8,128)} async-done(((f32[64,16,1024]{2,1,0:T(8,128)}), f32[64,16,1024]{2,1,0:T(8,128)}, u32[]{:S(2)}, u32[]{:S(2)}) %all-to-all-start.3) | async-done | bytes 4194336 | tf_op jit(solution)/shard_map/all_to_all | solution.py:130
  263.3 2.9 %gather_fusion.1 = f32[32,16,1024]{2,1,0:T(8,128)S(1)} fusion(f32[64,16,1024]{2,1,0:T(8,128)} %all-to-all-done.3, s32[1024]{0:T(1024)S(1)} %pad_clamp_fusion), kind=kCustom, calls=%fused_computation.1 | custom fusion | bytes 4194432 | tf_op jit(solution)/shard_map/jit(_take)/gather | solution.py:138
  266.2 6.2 %fusion.1 = bf16[512,1024]{1,0:T(8,128)(2,1)} fusion(f32[32,16,1024]{2,1,0:T(8,128)S(1)} %gather_fusion.1, bf16[512,2048]{1,0:T(8,128)(2,1)} %all-gather.2.cloned.1.call-done, bf16[1024,2048]{1,0:T(8,128)(2,1)} %param.11, pred[512]{0:T(512)(128)(4,1)S(1)} %broadcast_in_dim.123), kind=kOutput, calls=%fused_computation.6 | convolution fusion | flops 2149056512 | bytes 9437696 | tf_op jit(solution)/shard_map/dot_general | solution.py:142
  (66 shorter events, 10.6 us)
Async XLA Ops:
  7.2 90.5 %copy-start = (bf16[8,1024,64]{1,2,0:T(8,128)(2,1)S(1)}, bf16[8,1024,64]{1,2,0:T(8,128)(2,1)}, u32[]{:S(2)}) copy-start(bf16[8,1024,64]{1,2,0:T(8,128)(2,1)} %param.12) | copy-start | bytes 3145732
  10.8 12.6 %copy-start.2 = (bf16[512,1024]{1,0:T(8,128)(2,1)S(1)}, bf16[512,1024]{1,0:T(8,128)(2,1)}, u32[]{:S(2)}) copy-start(bf16[512,1024]{1,0:T(8,128)(2,1)} %param.10) | copy-start | bytes 3145732
  12.3 27.5 %all-to-all-start = ((bf16[32,2,4224]{2,1,0:T(2,128)(2,1)}), bf16[32,2,4224]{2,1,0:T(2,128)(2,1)}, u32[]{:S(2)}, u32[]{:S(2)}) async-start(bf16[32,2,4224]{2,1,0:T(2,128)(2,1)} %all_to_all.17), calls=%async_computation.1 | async-start | bytes 1081344 | tf_op jit(solution)/shard_map/all_to_all | solution.py:64
  44.4 5.8 %copy-start.1 = (bf16[64,4224]{1,0:T(8,128)(2,1)S(1)}, bf16[64,4224]{1,0:T(8,128)(2,1)}, u32[]{:S(2)}) copy-start(bf16[64,4224]{1,0:T(8,128)(2,1)} %all_to_all.19) | copy-start | bytes 1622020
  44.4 6.2 %slice-start = ((bf16[64,4224]{1,0:T(8,128)(2,1)}), bf16[64,4096]{1,0:T(8,128)(2,1)S(1)}, s32[]{:S(2)}) async-start(bf16[64,4224]{1,0:T(8,128)(2,1)} %all_to_all.19), calls=%async_computation.8 | async-start | bytes 1048576 | tf_op jit(solution)/shard_map/slice | solution.py:73
  44.4 53.2 %all-to-all-start.1 = ((bf16[64,16,1024]{2,1,0:T(8,128)(2,1)}), bf16[64,16,1024]{2,1,0:T(8,128)(2,1)}, u32[]{:S(2)}, u32[]{:S(2)}) async-start(bf16[64,16,1024]{2,1,0:T(8,128)(2,1)} %bitcast.22), calls=%async_computation.2 | async-start | bytes 4194304 | tf_op jit(solution)/shard_map/all_to_all | solution.py:66
  50.1 1.0 copy-start.8
  50.1 85.8 %all-reduce.4.cloned.1.call-start = ((), (), s32[]{:S(2)}) async-start(), calls=%async_computation.7 | async-start | bytes 524288 | tf_op jit(solution)/shard_map/psum | solution.py:103
  50.6 1.7 copy-start.3
  51.1 7.8 %copy-start.4 = (bf16[1024,256,1]{1,0,2:T(8,128)(2,1)}, bf16[1024,256,1]{1,0,2:T(8,128)(2,1)S(1)}, u32[]{:S(2)}) copy-start(bf16[1024,256,1]{1,0,2:T(8,128)(2,1)S(1)} %reshape.288) | copy-start | bytes 1572868
  52.3 124.2 %reduce-scatter.2.cloned.1.call-start = ((), (), s32[]{:S(2)}) async-start(), calls=%async_computation.5 | async-start | bytes 4718592 | tf_op jit(solution)/shard_map/reduce_scatter | solution.py:31
  58.9 0.7 copy-start.6
  58.9 0.7 copy-start.7
  129.0 35.0 %all-to-all-start.2 = ((f32[64,16,256]{2,1,0:T(8,128)}), f32[64,16,256]{2,1,0:T(8,128)S(1)}, u32[]{:S(2)}, u32[]{:S(2)}) async-start(f32[64,16,256]{2,1,0:T(8,128)} %bitcast.7), calls=%async_computation.3 | async-start | bytes 2097152 | tf_op jit(solution)/shard_map/all_to_all | solution.py:123
  164.0 6.2 %copy-start.5 = (bf16[1024,256,1]{1,0,2:T(8,128)(2,1)S(1)}, bf16[1024,256,1]{1,0,2:T(8,128)(2,1)}, u32[]{:S(2)}) copy-start(bf16[1024,256,1]{1,0,2:T(8,128)(2,1)} %copy-done.4) | copy-start | bytes 1572868
  164.0 99.2 %all-to-all-start.3 = ((f32[64,16,1024]{2,1,0:T(8,128)}), f32[64,16,1024]{2,1,0:T(8,128)}, u32[]{:S(2)}, u32[]{:S(2)}) async-start(f32[64,16,1024]{2,1,0:T(8,128)} %bitcast.68), calls=%async_computation.4 | async-start | bytes 8388608 | tf_op jit(solution)/shard_map/all_to_all | solution.py:130
  169.3 96.8 %all-gather.2.cloned.1.call-start = ((), (), s32[]{:S(2)}) async-start(), calls=%async_computation.6 | async-start | bytes 2359296 | tf_op jit(solution)/shard_map/all_gather | solution.py:143
Sparse Core Ops, SparseCore 0:
  53.8 67.5 all-reduce.3
  124.0 39.7 reduce-scatter.1
  172.0 30.6 all-gather.1
